TPU v7x, 512 devices: a whole 4x8x8 slice. The times are simulated.
512 devices in a mesh: atom: 4 (over x), tm: 4 (over y_hi), wave: 32 (over y_lo, z, core).
Axes of the slice: x: 4, y: 8 (y_hi: 4, y_lo: 2; y = y_hi * 2 + y_lo), z: 8, core: 2. Of those that a mesh axis runs over, the one named last changes fastest.
Arguments:
- positions: float32 [64, 3, 8192], P('tm', None, ('atom', 'wave')), may hold values from 0 to 1
- species: int32 [8192], P('atom'), may hold values 0 or 1
- kx_index: int32 [16], replicated, may hold values from 1 to 16
- kyz_index: int32 [2, 4096], P(None, 'wave'), may hold values from -16 to 16
Outputs:
- spectra: float32 [3, 64, 16, 4096], P(None, None, ('atom', 'tm'), 'wave')
- densities: float32 [64, 2, 2, 16, 4096], P('tm', None, None, 'atom', 'wave')
Inputs may be any that keep to these rules, and one draw needn't show every extreme that they name: `species`: 0 marks an oxygen atom, 1 a hydrogen atom.
All inputs are finite; a program needn't handle non-finite values. No bound on the sum of `species` on one device may be relied on, other than what follows from the above.
Results may differ from a plain program's by a relative error of at most 0.0034.
Values sent between devices are 32-bit elements; how exact they have to be, the bound alone decides.
No kernel may reach another device: no remote copies, remote signals or barrier semaphores. Data moves between devices by JAX's collectives and lax.ppermute only.
A program may use at most 64 MiB of HBM per device.

v0:
```python
import math

import jax
import jax.numpy as jnp
from jax import lax
from jax.sharding import PartitionSpec as P

TWO_PI = 2.0 * math.pi


def copy_for_each(shard, axis):
    peers = lax.axis_size(axis)
    return lax.all_to_all(
        jnp.broadcast_to(shard[None], (peers, *shard.shape)), axis, 0, 0, tiled=True
    )


def joined_along(pieces, dim):
    pieces = jnp.moveaxis(pieces, 0, dim)
    dims = pieces.shape
    return pieces.reshape(*dims[:dim], dims[dim] * dims[dim + 1], *dims[dim + 2 :])


def gathered_copies(shard, axis, dim):
    pieces = copy_for_each(shard, axis)
    return joined_along(pieces, dim)


def cut_along(shard, dim, peers):
    dims = shard.shape
    pieces = shard.reshape(*dims[:dim], peers, dims[dim] // peers, *dims[dim + 1 :])
    return jnp.moveaxis(pieces, dim, 0)


def sent_and_summed(shard, axis, dim):
    pieces = cut_along(shard, dim, lax.axis_size(axis))
    arrived = lax.all_to_all(pieces, axis, split_axis=0, concat_axis=0, tiled=True)
    return arrived.sum(axis=0)


def frac_turns(values):
    return values - jnp.floor(values)


def hann_window(length):
    frame_steps = jnp.arange(length).astype(jnp.float32)
    return 0.5 - 0.5 * jnp.cos(TWO_PI / length * (frame_steps + 0.5))


def combine(products):
    real_part = products[:, 0, :, 0] - products[:, 1, :, 1]
    imag_part = -(products[:, 1, :, 0] + products[:, 0, :, 1])
    return jnp.stack([real_part, imag_part], axis=1)


def transform(series):
    length = series.shape[0]
    window = hann_window(length)
    energy = jnp.sum(window * window)
    weighted = series * window[:, None, None, None, None]
    frame_steps = jnp.arange(length)
    phase_turns = (frame_steps[:, None] * frame_steps[None, :] % length).astype(jnp.float32)
    dft_angle = TWO_PI / length * phase_turns
    cos_table = jnp.cos(dft_angle)
    sin_table = jnp.sin(dft_angle)
    real_part = weighted[:, :, 0]
    imag_part = weighted[:, :, 1]
    highest = lax.Precision.HIGHEST
    spec_real = jnp.einsum("ft,tsmj->fsmj", cos_table, real_part, precision=highest) + jnp.einsum(
        "ft,tsmj->fsmj", sin_table, imag_part, precision=highest
    )
    spec_imag = jnp.einsum("ft,tsmj->fsmj", cos_table, imag_part, precision=highest) - jnp.einsum(
        "ft,tsmj->fsmj", sin_table, real_part, precision=highest
    )
    oxygen_pair = spec_real[:, 0] * spec_real[:, 0] + spec_imag[:, 0] * spec_imag[:, 0]
    cross_pair = spec_real[:, 0] * spec_real[:, 1] + spec_imag[:, 0] * spec_imag[:, 1]
    hydrogen_pair = spec_real[:, 1] * spec_real[:, 1] + spec_imag[:, 1] * spec_imag[:, 1]
    return jnp.stack([oxygen_pair, cross_pair, hydrogen_pair]) / energy


def local(positions, species, kx_index, kyz_index):
    local_frames = positions.shape[0]
    kx_count = kx_index.shape[0]
    kyz_local = kyz_index.shape[1]
    total_atoms = positions.shape[2] * lax.axis_size("atom") * lax.axis_size("wave")
    onehot_all = jnp.stack([species == 0, species == 1]).astype(jnp.float32)
    kx_real = kx_index.astype(jnp.float32)
    ky_real = kyz_index[0].astype(jnp.float32)
    kz_real = kyz_index[1].astype(jnp.float32)
    block_coords = gathered_copies(positions, "wave", 2)
    atom_count = block_coords.shape[2]
    x_angle = TWO_PI * frac_turns(block_coords[:, 0][:, None, :] * kx_real[None, :, None])
    phases = jnp.stack([jnp.cos(x_angle), jnp.sin(x_angle)], axis=1)
    x_table = (onehot_all[None, :, None, None, :] * phases[:, None]).astype(jnp.bfloat16)
    x_table = x_table.reshape(local_frames, 4 * kx_count, atom_count)
    y_angle = TWO_PI * frac_turns(block_coords[:, 1][:, :, None] * ky_real[None, None, :])
    z_angle = TWO_PI * frac_turns(block_coords[:, 2][:, :, None] * kz_real[None, None, :])
    cy = jnp.cos(y_angle)
    sy = jnp.sin(y_angle)
    cz = jnp.cos(z_angle)
    sz = jnp.sin(z_angle)
    yz_cos = cy * cz - sy * sz
    yz_sin = sy * cz + cy * sz
    yz_table = jnp.concatenate([yz_cos, yz_sin], axis=2).astype(jnp.bfloat16)
    products = lax.dot_general(
        x_table, yz_table, (((2,), (1,)), ((0,), (0,))), preferred_element_type=jnp.float32
    )
    products = products.reshape(local_frames, 2, 2, kx_count, 2, kyz_local)
    partial_value = jax.vmap(combine)(products)
    owned = sent_and_summed(partial_value, "atom", 3)
    densities = owned / jnp.sqrt(jnp.float32(total_atoms))
    spectra = transform(lax.all_to_all(densities, "tm", split_axis=3, concat_axis=0, tiled=True))
    return (spectra, densities)


def solution(mesh):
    in_specs = (P("tm", None, ("atom", "wave")), P("atom"), P(), P(None, "wave"))
    out_specs = (P(None, None, ("atom", "tm"), "wave"), P("tm", None, None, "atom", "wave"))
    return jax.shard_map(local, mesh=mesh, in_specs=in_specs, out_specs=out_specs, check_vma=False)
```

profile of v0, /device:TPU:72, one launch (start us, length us, event | category | flops | bytes accessed | tf_op | source)
XLA Modules:
  0.0 202.7 jit_solution(4754116451197903972)
XLA Ops:
  0.6 0.7 copy-done
  1.4 1.2 reshape.363
  2.7 11.0 %all-to-all-start = ((f32[32,1,3072]{2,1,0:T(1,128)}), f32[32,1,3072]{2,1,0:T(1,128)S(1)}, u32[]{:S(2)}, u32[]{:S(2)}) async-start(f32[32,1,3072]{2,1,0:T(1,128)} %reshape.363), calls=%async_computation | async-start | bytes 786432 | tf_op jit(solution)/shard_map/all_to_all | solution.py:13
  13.7 0.7 convert_element_type.55
  14.4 0.7 broadcast_compare_fusion.1
  15.1 0.8 convert_bitcast_fusion.1
  15.9 11.6 %all-to-all-done = f32[32,1,3072]{2,1,0:T(1,128)S(1)} async-done(((f32[32,1,3072]{2,1,0:T(1,128)}), f32[32,1,3072]{2,1,0:T(1,128)S(1)}, u32[]{:S(2)}, u32[]{:S(2)}) %all-to-all-start) | async-done | bytes 393248 | tf_op jit(solution)/shard_map/all_to_all | solution.py:13
  27.5 0.5 broadcast.110
  28.0 1.6 reduce
  30.5 7.5 %fusion.13 = (f32[16,1,16,2048]{3,2,1,0:T(8,128)S(1)}, f32[16,1,16,2048]{3,2,1,0:T(8,128)S(1)}) fusion(f32[16]{0:T(128)S(1)} %convert_element_type.55, f32[16,2048]{1,0:T(8,128)S(1)} %get-tuple-element.16), kind=kLoop, calls=%fused_computation.20 | loop fusion | flops 2097152 | bytes 4325440 | tf_op jit(solution)/shard_map/cos | solution.py:93
  38.0 0.5 pad_maximum_fusion
  38.5 1.1 fusion.10
  39.7 124.7 %subtract_convert_fusion = (bf16[16,2048,128]{2,1,0:T(8,128)(2,1)S(1)}, bf16[16,2048,128]{2,1,0:T(8,128)(2,1)S(1)}) fusion(f32[128]{0:T(128)S(1)} %get-tuple-element.26, f32[16,2048]{1,0:T(8,128)S(1)} %get-tuple-element.15, f32[128]{0:T(128)S(1)} %get-tuple-element.25, f32[16,2048]{1,0:T(8,128)S(1)} %get-tuple-element.14), kind=kLoop, calls=%fused_computation.9 | loop fusion | flops 67108864 | bytes 17040384 | tf_op jit(solution)/shard_map/convert
  164.4 3.8 %fusion.2 = f32[16,64,256]{2,1,0:T(8,128)S(1)} fusion(bf16[16,64,2048]{2,1,0:T(8,128)(2,1)S(1)} %fusion.10, bf16[16,2048,128]{2,1,0:T(8,128)(2,1)S(1)} %get-tuple-element.18, bf16[16,2048,128]{2,1,0:T(8,128)(2,1)S(1)} %get-tuple-element.17), kind=kOutput, calls=%fused_computation.4 | convolution fusion | flops 1107296256 | bytes 22020096 | tf_op jit(solution)/shard_map/dot_general | solution.py:105
  168.2 0.5 reshape.358
  168.7 1.1 fusion.54
  169.9 0.6 fusion.15
  170.7 13.6 %all_to_all.28 = f32[4,16,2,2,4,128]{5,4,2,1,3,0:T(4,128)S(1)} all-to-all(f32[4,16,2,2,4,128]{5,4,2,1,3,0:T(4,128)S(1)} %copy.38), channel_id=1, replica_groups=mesh['atom'=4,'tm'=4,'wave'=32] {'atom'}, dimensions={0} | all-to-all | bytes 1048576 | tf_op jit(solution)/shard_map/all_to_all | solution.py:37
  184.5 0.7 copy.40
  185.1 6.2 %all-to-all-start.2 = ((f32[16,2,2,4,128]{4,0,2,1,3:T(8,128)}), f32[16,2,2,4,128]{4,0,2,1,3:T(8,128)S(1)}, u32[]{:S(2)}, u32[]{:S(2)}) async-start(f32[16,2,2,4,128]{4,0,2,1,3:T(8,128)} %copy.40), calls=%async_computation.2 | async-start | bytes 262144 | tf_op jit(solution)/shard_map/all_to_all | solution.py:112
  191.4 0.7 multiply_reduce_fusion
  192.1 0.7 copy.46
  192.8 7.1 %all-to-all-done.2 = f32[16,2,2,4,128]{4,0,2,1,3:T(8,128)S(1)} async-done(((f32[16,2,2,4,128]{4,0,2,1,3:T(8,128)}), f32[16,2,2,4,128]{4,0,2,1,3:T(8,128)S(1)}, u32[]{:S(2)}, u32[]{:S(2)}) %all-to-all-start.2) | async-done | bytes 131104 | tf_op jit(solution)/shard_map/all_to_all | solution.py:112
  201.4 1.3 maximum_divide_fusion
  (24 shorter events, 2.9 us)
Async XLA Ops:
  0.6 0.7 copy-start
  2.7 24.8 %all-to-all-start = ((f32[32,1,3072]{2,1,0:T(1,128)}), f32[32,1,3072]{2,1,0:T(1,128)S(1)}, u32[]{:S(2)}, u32[]{:S(2)}) async-start(f32[32,1,3072]{2,1,0:T(1,128)} %reshape.363), calls=%async_computation | async-start | bytes 786432 | tf_op jit(solution)/shard_map/all_to_all | solution.py:13
  185.1 14.7 %all-to-all-start.2 = ((f32[16,2,2,4,128]{4,0,2,1,3:T(8,128)}), f32[16,2,2,4,128]{4,0,2,1,3:T(8,128)S(1)}, u32[]{:S(2)}, u32[]{:S(2)}) async-start(f32[16,2,2,4,128]{4,0,2,1,3:T(8,128)} %copy.40), calls=%async_computation.2 | async-start | bytes 262144 | tf_op jit(solution)/shard_map/all_to_all | solution.py:112
where the time goes:
time: 203 us
  other arithmetic  140 us (69%)
  waiting for transfers between devices  18.7 us (9%)
  starting transfers between devices  17.3 us (9%)
  blocking collectives  13.6 us (7%)
  local copies, waits for them, and re-layouts  6.68 us (3%)
  matrix products  5.13 us (3%)
    another operation x1, other arithmetic  125 us
    all_to_all x1, blocking collectives, sent_and_summed(): lax.all_to_all(pieces, axis, split_axis=0, concat_axis=0, tiled=True)  13.6 us
    all_to_all x1, waiting for transfers between devices, copy_for_each(): lax.all_to_all(jnp.broadcast_to(shard[None], (peers, *shard.shape)), axis...  11.6 us
    all_to_all x1, starting transfers between devices, copy_for_each(): lax.all_to_all(jnp.broadcast_to(shard[None], (peers, *shard.shape)), axis...  11 us
    cos x1, other arithmetic, local(): phases = jnp.stack([jnp.cos(x_angle), jnp.sin(x_angle)], axis=1)  7.5 us
    all_to_all x1, waiting for transfers between devices, local(): lax.all_to_all(densities, 'tm', split_axis=3, concat_axis=0, tiled=True)  7.12 us
    all_to_all x1, starting transfers between devices, local(): lax.all_to_all(densities, 'tm', split_axis=3, concat_axis=0, tiled=True)  6.22 us
  transfers between devices with their start and end apart: 2, of which 2 were waited for; matrix products, arithmetic and copies ran while one was open for 2% of the time, Pallas kernels for 0%

commit v1 on v0

--- a/solution.py
+++ b/solution.py
@@ -3,6 +3,8 @@
 import jax
 import jax.numpy as jnp
 from jax import lax
+from jax.experimental import pallas as pl
+from jax.experimental.pallas import tpu as pltpu
 from jax.sharding import PartitionSpec as P
 
 TWO_PI = 2.0 * math.pi
@@ -78,35 +80,105 @@
     return jnp.stack([oxygen_pair, cross_pair, hydrogen_pair]) / energy
 
 
+def power_rows(base_cos, base_sin, count):
+    rows = [(jnp.ones_like(base_cos), jnp.zeros_like(base_sin)), (base_cos, base_sin)]
+    for _ in range(count - 1):
+        prev_cos, prev_sin = rows[-1]
+        rows.append((prev_cos * base_cos - prev_sin * base_sin, prev_sin * base_cos + prev_cos * base_sin))
+    return rows
+
+
+def split_dot(picks, table):
+    high = table.astype(jnp.bfloat16)
+    low = (table - high.astype(jnp.float32)).astype(jnp.bfloat16)
+    dims = (((1,), (0,)), ((), ()))
+    return lax.dot_general(picks, high, dims, preferred_element_type=jnp.float32) + lax.dot_general(
+        picks, low, dims, preferred_element_type=jnp.float32
+    )
+
+
+def frame_kernel(base_ref, onehot_ref, pick_x_ref, pick_y_ref, pick_z_ref, out_ref, axis_ref, x_ref):
+    base = base_ref[0]
+    kmax = 16
+    rows_pad = axis_ref.shape[1]
+    for axis in range(2):
+        powers = power_rows(base[2 + 2 * axis : 3 + 2 * axis], base[3 + 2 * axis : 4 + 2 * axis], kmax)
+        for k, (cos_k, sin_k) in enumerate(powers):
+            axis_ref[2 * axis, kmax + k : kmax + k + 1, :] = cos_k
+            axis_ref[2 * axis + 1, kmax + k : kmax + k + 1, :] = sin_k
+            if k:
+                axis_ref[2 * axis, kmax - k : kmax - k + 1, :] = cos_k
+                axis_ref[2 * axis + 1, kmax - k : kmax - k + 1, :] = -sin_k
+        pad = rows_pad - (2 * kmax + 1)
+        zeros = jnp.zeros((pad, base.shape[1]), jnp.float32)
+        axis_ref[2 * axis, 2 * kmax + 1 :, :] = zeros
+        axis_ref[2 * axis + 1, 2 * kmax + 1 :, :] = zeros
+    x_powers = power_rows(base[0:1], base[1:2], kmax)
+    for k in range(1, kmax + 1):
+        x_ref[0, k - 1 : k, :] = x_powers[k][0]
+        x_ref[1, k - 1 : k, :] = x_powers[k][1]
+    pick_x = pick_x_ref[...]
+    pick_y = pick_y_ref[...]
+    pick_z = pick_z_ref[...]
+    cy = split_dot(pick_y, axis_ref[0])
+    sy = split_dot(pick_y, axis_ref[1])
+    cz = split_dot(pick_z, axis_ref[2])
+    sz = split_dot(pick_z, axis_ref[3])
+    yz_cos = (cy * cz - sy * sz).astype(jnp.bfloat16)
+    yz_sin = (sy * cz + cy * sz).astype(jnp.bfloat16)
+    x_cos = split_dot(pick_x, x_ref[0])
+    x_sin = split_dot(pick_x, x_ref[1])
+    onehot = onehot_ref[...]
+    x_table = jnp.concatenate(
+        [onehot[0:1] * x_cos, onehot[0:1] * x_sin, onehot[1:2] * x_cos, onehot[1:2] * x_sin], axis=0
+    ).astype(jnp.bfloat16)
+    dims = (((1,), (1,)), ((), ()))
+    with_cos = lax.dot_general(x_table, yz_cos, dims, preferred_element_type=jnp.float32)
+    with_sin = lax.dot_general(x_table, yz_sin, dims, preferred_element_type=jnp.float32)
+    kx = kmax
+    for s in range(2):
+        cos_rows = slice((2 * s) * kx, (2 * s + 1) * kx)
+        sin_rows = slice((2 * s + 1) * kx, (2 * s + 2) * kx)
+        out_ref[0, s, 0] = with_cos[cos_rows] - with_sin[sin_rows]
+        out_ref[0, s, 1] = -(with_sin[cos_rows] + with_cos[sin_rows])
+
+
+def picks_of(index, lowest, count):
+    cols = jnp.arange(count, dtype=jnp.int32)
+    return (index[:, None] - lowest == cols[None, :]).astype(jnp.bfloat16)
+
+
 def local(positions, species, kx_index, kyz_index):
     local_frames = positions.shape[0]
     kx_count = kx_index.shape[0]
     kyz_local = kyz_index.shape[1]
     total_atoms = positions.shape[2] * lax.axis_size("atom") * lax.axis_size("wave")
     onehot_all = jnp.stack([species == 0, species == 1]).astype(jnp.float32)
-    kx_real = kx_index.astype(jnp.float32)
-    ky_real = kyz_index[0].astype(jnp.float32)
-    kz_real = kyz_index[1].astype(jnp.float32)
     block_coords = gathered_copies(positions, "wave", 2)
     atom_count = block_coords.shape[2]
-    x_angle = TWO_PI * frac_turns(block_coords[:, 0][:, None, :] * kx_real[None, :, None])
-    phases = jnp.stack([jnp.cos(x_angle), jnp.sin(x_angle)], axis=1)
-    x_table = (onehot_all[None, :, None, None, :] * phases[:, None]).astype(jnp.bfloat16)
-    x_table = x_table.reshape(local_frames, 4 * kx_count, atom_count)
-    y_angle = TWO_PI * frac_turns(block_coords[:, 1][:, :, None] * ky_real[None, None, :])
-    z_angle = TWO_PI * frac_turns(block_coords[:, 2][:, :, None] * kz_real[None, None, :])
-    cy = jnp.cos(y_angle)
-    sy = jnp.sin(y_angle)
-    cz = jnp.cos(z_angle)
-    sz = jnp.sin(z_angle)
-    yz_cos = cy * cz - sy * sz
-    yz_sin = sy * cz + cy * sz
-    yz_table = jnp.concatenate([yz_cos, yz_sin], axis=2).astype(jnp.bfloat16)
-    products = lax.dot_general(
-        x_table, yz_table, (((2,), (1,)), ((0,), (0,))), preferred_element_type=jnp.float32
-    )
-    products = products.reshape(local_frames, 2, 2, kx_count, 2, kyz_local)
-    partial_value = jax.vmap(combine)(products)
+    angle = TWO_PI * frac_turns(block_coords)
+    base = jnp.stack([jnp.cos(angle), jnp.sin(angle)], axis=2).reshape(local_frames, 6, atom_count)
+    rows_pad = 48
+    pick_x = picks_of(kx_index, 1, 16)
+    pick_y = picks_of(kyz_index[0], -16, rows_pad)
+    pick_z = picks_of(kyz_index[1], -16, rows_pad)
+    partial_value = pl.pallas_call(
+        frame_kernel,
+        grid=(local_frames,),
+        in_specs=[
+            pl.BlockSpec((1, 6, atom_count), lambda t: (t, 0, 0)),
+            pl.BlockSpec((2, atom_count), lambda t: (0, 0)),
+            pl.BlockSpec((kx_count, 16), lambda t: (0, 0)),
+            pl.BlockSpec((kyz_local, rows_pad), lambda t: (0, 0)),
+            pl.BlockSpec((kyz_local, rows_pad), lambda t: (0, 0)),
+        ],
+        out_specs=pl.BlockSpec((1, 2, 2, kx_count, kyz_local), lambda t: (t, 0, 0, 0, 0)),
+        out_shape=jax.ShapeDtypeStruct((local_frames, 2, 2, kx_count, kyz_local), jnp.float32),
+        scratch_shapes=[
+            pltpu.VMEM((4, rows_pad, atom_count), jnp.float32),
+            pltpu.VMEM((2, 16, atom_count), jnp.float32),
+        ],
+    )(base, onehot_all, pick_x, pick_y, pick_z)
     owned = sent_and_summed(partial_value, "atom", 3)
     densities = owned / jnp.sqrt(jnp.float32(total_atoms))
     spectra = transform(lax.all_to_all(densities, "tm", split_axis=3, concat_axis=0, tiled=True))

time: 203 us -> 113 us (0.56)
  the two profiles are of different devices: /device:TPU:72 before, /device:TPU:8 now
where the time goes in v1:
time: 113 us; the launch traced here: 112 us
  Pallas kernels  45.6 us (40%)
  starting transfers between devices  18.3 us (16%)
  waiting for transfers between devices  17.7 us (16%)
  blocking collectives  13.4 us (12%)
  local copies, waits for them, and re-layouts  7.95 us (7%)
  other arithmetic  7.2 us (6%)
  matrix products  1.33 us (1%)
    pallas_call x1, Pallas kernels, local(): pl.pallas_call(frame_kernel, grid=(local_frames,), in_specs=[pl.BlockSpec...  45.6 us
    all_to_all x1, blocking collectives, sent_and_summed(): lax.all_to_all(pieces, axis, split_axis=0, concat_axis=0, tiled=True)  13.4 us
    all_to_all x1, starting transfers between devices, copy_for_each(): lax.all_to_all(jnp.broadcast_to(shard[None], (peers, *shard.shape)), axis...  12.1 us
    all_to_all x1, waiting for transfers between devices, copy_for_each(): lax.all_to_all(jnp.broadcast_to(shard[None], (peers, *shard.shape)), axis...  10 us
    all_to_all x1, waiting for transfers between devices, local(): lax.all_to_all(densities, 'tm', split_axis=3, concat_axis=0, tiled=True)  7.68 us
    all_to_all x1, starting transfers between devices, local(): lax.all_to_all(densities, 'tm', split_axis=3, concat_axis=0, tiled=True)  6.19 us
    unnamed x13, local copies, waits for them, and re-layouts  3.54 us
  transfers between devices with their start and end apart: 2, of which 2 were waited for; matrix products, arithmetic and copies ran while one was open for 2% of the time, Pallas kernels for 0%

profile of v1, /device:TPU:8, one launch (start us, length us, event | category | flops | bytes accessed | tf_op | source)
XLA Modules:
  0.0 112.3 jit_solution(9301595202757427316)
XLA Ops:
  0.6 0.7 copy-done
  1.4 1.2 %reshape.321 = f32[32,1,3072]{2,1,0:T(1,128)} reshape(f32[32,3,16,64]{3,2,1,0:T(8,128)S(1)} %broadcast_bitcast_fusion) | data formatting | bytes 786432
  2.7 12.1 %all-to-all-start = ((f32[32,1,3072]{2,1,0:T(1,128)}), f32[32,1,3072]{2,1,0:T(1,128)S(1)}, u32[]{:S(2)}, u32[]{:S(2)}) async-start(f32[32,1,3072]{2,1,0:T(1,128)} %reshape.321), calls=%async_computation | async-start | bytes 786432 | tf_op jit(solution)/shard_map/all_to_all | solution.py:15
  14.8 0.7 copy-done.3
  15.4 0.6 copy-done.4
  16.1 0.7 fusion.27.pick_x_ref
  16.8 0.6 add_convert_fusion.onehot_ref
  17.4 0.7 fusion.4
  18.1 10.0 %all-to-all-done = f32[32,1,3072]{2,1,0:T(1,128)S(1)} async-done(((f32[32,1,3072]{2,1,0:T(1,128)}), f32[32,1,3072]{2,1,0:T(1,128)S(1)}, u32[]{:S(2)}, u32[]{:S(2)}) %all-to-all-start) | async-done | bytes 393248 | tf_op jit(solution)/shard_map/all_to_all | solution.py:15
  28.2 0.5 broadcast.106
  28.7 1.5 %reduce = f32[32,3072]{1,0:T(8,128)S(1)} reduce(f32[32,1,3072]{2,1,0:T(1,128)S(1)} %all-to-all-done, f32[]{:T(128)} %broadcast.106), dimensions={1}, to_apply=%all_to_all.19.reduce_sub_computation | reduce | bytes 786436 | tf_op jit(solution)/shard_map/all_to_all | solution.py:15
  31.0 1.5 %fusion.3 = (f32[16,3,1,2048]{3,0,2,1:T(8,128)S(1)}, f32[16,3,1,2048]{3,0,2,1:T(8,128)S(1)}) fusion(f32[16,3,1,2048]{3,0,2,1:T(8,128)S(1)} %reshape.314), kind=kLoop, calls=%fused_computation.8 | loop fusion | flops 294912 | bytes 1179648 | tf_op jit(solution)/shard_map/cos | solution.py:160
  32.5 1.4 %copy.28.base_ref = f32[16,6,2048]{2,1,0:T(8,128)} copy(f32[16,6,2048]{2,0,1:T(8,128)S(1)} %bitcast.63) | data formatting | bytes 1572864 | tf_op jit(solution)/shard_map/reshape | solution.py:160
  34.0 45.6 %shard_map.59 = f32[16,2,2,16,128]{4,3,2,1,0:T(8,128)} custom-call(f32[16,6,2048]{2,1,0:T(8,128)} %copy.28.base_ref, f32[2,2048]{1,0:T(2,128)} %add_convert_fusion.onehot_ref, bf16[16,16]{1,0:T(8,128)(2,1)} %fusion.27.pick_x_ref, bf16[128,48]{1,0:T(8,128)(2,1)} %get-tuple-element.18.pick_y_ref, bf16[128,48]{1,0:T(8,128)(2,1)} %get-tuple-element.19.pick_z_ref), custom_call_target="tpu_custom_call" | custom-call | tf_op jit(solution)/shard_map/pallas_call | solution.py:165
  79.6 1.1 %copy.37 = f32[16,2,2,4,4,128]{5,4,2,1,0,3:T(4,128)S(1)} copy(f32[16,2,2,4,4,128]{5,4,3,2,1,0:T(4,128)} %bitcast.64) | data formatting | bytes 1048576 | tf_op jit(solution)/shard_map/reshape | solution.py:33
  80.7 13.4 %all_to_all.28 = f32[4,16,2,2,4,128]{5,4,3,2,1,0:T(4,128)S(1)} all-to-all(f32[4,16,2,2,4,128]{5,4,3,2,1,0:T(4,128)S(1)} %bitcast.65), channel_id=1, replica_groups=mesh['atom'=4,'tm'=4,'wave'=32] {'atom'}, dimensions={0} | all-to-all | bytes 1048576 | tf_op jit(solution)/shard_map/all_to_all | solution.py:39
  94.3 0.7 copy.30
  95.0 6.2 %all-to-all-start.2 = ((f32[16,2,2,4,128]{4,0,2,1,3:T(8,128)}), f32[16,2,2,4,128]{4,0,2,1,3:T(8,128)S(1)}, u32[]{:S(2)}, u32[]{:S(2)}) async-start(f32[16,2,2,4,128]{4,0,2,1,3:T(8,128)} %copy.30), calls=%async_computation.2 | async-start | bytes 262144 | tf_op jit(solution)/shard_map/all_to_all | solution.py:184
  101.2 0.7 multiply_reduce_fusion
  101.9 7.7 %all-to-all-done.2 = f32[16,2,2,4,128]{4,0,2,1,3:T(8,128)S(1)} async-done(((f32[16,2,2,4,128]{4,0,2,1,3:T(8,128)}), f32[16,2,2,4,128]{4,0,2,1,3:T(8,128)S(1)}, u32[]{:S(2)}, u32[]{:S(2)}) %all-to-all-start.2) | async-done | bytes 131104 | tf_op jit(solution)/shard_map/all_to_all | solution.py:184
  109.7 0.3 fusion.7
  110.4 0.3 fusion
  110.7 0.3 convolution_add_fusion
  111.1 1.2 %maximum_divide_fusion = f32[3,64,1,128]{3,1,2,0:T(8,128)} fusion(f32[1,64,1,128]{3,1,2,0:T(8,128)S(1)} %fusion.11, f32[1,64,1,128]{3,1,2,0:T(8,128)S(1)} %get-tuple-element.13, f32[1,64,1,128]{3,1,2,0:T(8,128)S(1)} %get-tuple-element.12, f32[]{:T(128)} %multiply_reduce_fusion), kind=kLoop, calls=%fused_computation.9 | loop fusion | flops 73728 | bytes 196612 | tf_op jit(solution)/shard_map/div | solution.py:80
  (26 shorter events, 1.6 us)
Async XLA Ops:
  0.6 0.7 copy-start
  2.7 12.1 %copy-start.2 = (s32[2048]{0:T(1024)S(1)}, s32[2048]{0:T(1024)}, u32[]{:S(2)}) copy-start(s32[2048]{0:T(1024)} %param.5) | copy-start | bytes 24580
  2.7 25.5 %all-to-all-start = ((f32[32,1,3072]{2,1,0:T(1,128)}), f32[32,1,3072]{2,1,0:T(1,128)S(1)}, u32[]{:S(2)}, u32[]{:S(2)}) async-start(f32[32,1,3072]{2,1,0:T(1,128)} %reshape.321), calls=%async_computation | async-start | bytes 786432 | tf_op jit(solution)/shard_map/all_to_all | solution.py:15
  14.7 0.7 copy-start.3
  15.4 0.7 copy-start.4
  94.3 0.7 copy-start.1
  95.0 14.6 %all-to-all-start.2 = ((f32[16,2,2,4,128]{4,0,2,1,3:T(8,128)}), f32[16,2,2,4,128]{4,0,2,1,3:T(8,128)S(1)}, u32[]{:S(2)}, u32[]{:S(2)}) async-start(f32[16,2,2,4,128]{4,0,2,1,3:T(8,128)} %copy.30), calls=%async_computation.2 | async-start | bytes 262144 | tf_op jit(solution)/shard_map/all_to_all | solution.py:184

commit v2 on v1

--- a/solution.py
+++ b/solution.py
@@ -88,16 +88,16 @@
     return rows
 
 
-def split_dot(picks, table):
+def split_dot(picks, table, stacked):
+    rows = table.shape[0]
     high = table.astype(jnp.bfloat16)
-    low = (table - high.astype(jnp.float32)).astype(jnp.bfloat16)
+    stacked[0:rows, :] = high
+    stacked[rows : 2 * rows, :] = (table - high.astype(jnp.float32)).astype(jnp.bfloat16)
     dims = (((1,), (0,)), ((), ()))
-    return lax.dot_general(picks, high, dims, preferred_element_type=jnp.float32) + lax.dot_general(
-        picks, low, dims, preferred_element_type=jnp.float32
-    )
+    return lax.dot_general(picks, stacked[...], dims, preferred_element_type=jnp.float32)
 
 
-def frame_kernel(base_ref, onehot_ref, pick_x_ref, pick_y_ref, pick_z_ref, out_ref, axis_ref, x_ref):
+def frame_kernel(base_ref, onehot_ref, pick_x_ref, pick_y_ref, pick_z_ref, out_ref, axis_ref, x_ref, yz_half, x_half):
     base = base_ref[0]
     kmax = 16
     rows_pad = axis_ref.shape[1]
@@ -120,14 +120,14 @@
     pick_x = pick_x_ref[...]
     pick_y = pick_y_ref[...]
     pick_z = pick_z_ref[...]
-    cy = split_dot(pick_y, axis_ref[0])
-    sy = split_dot(pick_y, axis_ref[1])
-    cz = split_dot(pick_z, axis_ref[2])
-    sz = split_dot(pick_z, axis_ref[3])
+    cy = split_dot(pick_y, axis_ref[0], yz_half.at[0])
+    sy = split_dot(pick_y, axis_ref[1], yz_half.at[1])
+    cz = split_dot(pick_z, axis_ref[2], yz_half.at[2])
+    sz = split_dot(pick_z, axis_ref[3], yz_half.at[3])
     yz_cos = (cy * cz - sy * sz).astype(jnp.bfloat16)
     yz_sin = (sy * cz + cy * sz).astype(jnp.bfloat16)
-    x_cos = split_dot(pick_x, x_ref[0])
-    x_sin = split_dot(pick_x, x_ref[1])
+    x_cos = split_dot(pick_x, x_ref[0], x_half.at[0])
+    x_sin = split_dot(pick_x, x_ref[1], x_half.at[1])
     onehot = onehot_ref[...]
     x_table = jnp.concatenate(
         [onehot[0:1] * x_cos, onehot[0:1] * x_sin, onehot[1:2] * x_cos, onehot[1:2] * x_sin], axis=0
@@ -145,7 +145,8 @@
 
 def picks_of(index, lowest, count):
     cols = jnp.arange(count, dtype=jnp.int32)
-    return (index[:, None] - lowest == cols[None, :]).astype(jnp.bfloat16)
+    picks = (index[:, None] - lowest == cols[None, :]).astype(jnp.bfloat16)
+    return jnp.concatenate([picks, picks], axis=1)
 
 
 def local(positions, species, kx_index, kyz_index):
@@ -154,7 +155,7 @@
     kyz_local = kyz_index.shape[1]
     total_atoms = positions.shape[2] * lax.axis_size("atom") * lax.axis_size("wave")
     onehot_all = jnp.stack([species == 0, species == 1]).astype(jnp.float32)
-    block_coords = gathered_copies(positions, "wave", 2)
+    block_coords = lax.all_gather(positions, "wave", axis=2, tiled=True)
     atom_count = block_coords.shape[2]
     angle = TWO_PI * frac_turns(block_coords)
     base = jnp.stack([jnp.cos(angle), jnp.sin(angle)], axis=2).reshape(local_frames, 6, atom_count)
@@ -168,18 +169,20 @@
         in_specs=[
             pl.BlockSpec((1, 6, atom_count), lambda t: (t, 0, 0)),
             pl.BlockSpec((2, atom_count), lambda t: (0, 0)),
-            pl.BlockSpec((kx_count, 16), lambda t: (0, 0)),
-            pl.BlockSpec((kyz_local, rows_pad), lambda t: (0, 0)),
-            pl.BlockSpec((kyz_local, rows_pad), lambda t: (0, 0)),
+            pl.BlockSpec((kx_count, 32), lambda t: (0, 0)),
+            pl.BlockSpec((kyz_local, 2 * rows_pad), lambda t: (0, 0)),
+            pl.BlockSpec((kyz_local, 2 * rows_pad), lambda t: (0, 0)),
         ],
         out_specs=pl.BlockSpec((1, 2, 2, kx_count, kyz_local), lambda t: (t, 0, 0, 0, 0)),
         out_shape=jax.ShapeDtypeStruct((local_frames, 2, 2, kx_count, kyz_local), jnp.float32),
         scratch_shapes=[
             pltpu.VMEM((4, rows_pad, atom_count), jnp.float32),
             pltpu.VMEM((2, 16, atom_count), jnp.float32),
+            pltpu.VMEM((4, 2 * rows_pad, atom_count), jnp.bfloat16),
+            pltpu.VMEM((2, 32, atom_count), jnp.bfloat16),
         ],
     )(base, onehot_all, pick_x, pick_y, pick_z)
-    owned = sent_and_summed(partial_value, "atom", 3)
+    owned = lax.psum_scatter(partial_value, "atom", scatter_dimension=3, tiled=True)
     densities = owned / jnp.sqrt(jnp.float32(total_atoms))
     spectra = transform(lax.all_to_all(densities, "tm", split_axis=3, concat_axis=0, tiled=True))
     return (spectra, densities)

time: 113 us -> 162 us (1.43)
  blocking collectives: 13.4 us -> 54.2 us
  between operations: 0.82 us -> 14.2 us
  waiting for transfers between devices: 17.7 us -> 31 us
  starting transfers between devices: 18.3 us -> 5.87 us
  Pallas kernels: 45.6 us -> 38.6 us
    all_gather x0 -> x1, blocking collectives: none -> 54.2 us  [local(): block_coords = lax.all_gather(positions, 'wave', axis=2, tiled=True)]
    reduce_scatter x0 -> x1, waiting for transfers between devices: none -> 23.4 us  [local(): lax.psum_scatter(partial_value, 'atom', scatter_dimension=3, tiled=True)]
    all_to_all x1 -> x0, blocking collectives: 13.4 us -> none  [sent_and_summed(): lax.all_to_all(pieces, axis, split_axis=0, concat_axis=0, tiled=True)]
    all_to_all x1 -> x0, starting transfers between devices: 12.1 us -> none  [copy_for_each(): lax.all_to_all(jnp.broadcast_to(shard[None], (peers, *shard.shape)), axis...]
    all_to_all x1 -> x0, waiting for transfers between devices: 10 us -> none  [copy_for_each(): lax.all_to_all(jnp.broadcast_to(shard[None], (peers, *shard.shape)), axis...]
    pallas_call x1, Pallas kernels: 45.6 us -> 38.6 us  [local(): pl.pallas_call(frame_kernel, grid=(local_frames,), in_specs=[pl.BlockSpec...]
    all_gather x0 -> x1, local copies, waits for them, and re-layouts: none -> 3.35 us  [local(): block_coords = lax.all_gather(positions, 'wave', axis=2, tiled=True)]
    pallas_call x0 -> x1, local copies, waits for them, and re-layouts: none -> 2.14 us  [local(): pl.pallas_call(frame_kernel, grid=(local_frames,), in_specs=[pl.BlockSpec...]
  transfers between devices with their start and end apart: 2 -> 2, of which waited for: 2 -> 2; matrix products, arithmetic and copies ran while one was open for 2% -> 1% of each run, Pallas kernels for 0% -> 0%
where the time goes in v2:
time: 162 us
  blocking collectives  54.2 us (33%)
  Pallas kernels  38.6 us (24%)
  waiting for transfers between devices  31 us (19%)
  between operations  14.2 us (9%)
  local copies, waits for them, and re-layouts  9.28 us (6%)
  other arithmetic  7.44 us (5%)
  starting transfers between devices  5.87 us (4%)
    all_gather x1, blocking collectives, local(): block_coords = lax.all_gather(positions, 'wave', axis=2, tiled=True)  54.2 us
    pallas_call x1, Pallas kernels, local(): pl.pallas_call(frame_kernel, grid=(local_frames,), in_specs=[pl.BlockSpec...  38.6 us
    reduce_scatter x1, waiting for transfers between devices, local(): lax.psum_scatter(partial_value, 'atom', scatter_dimension=3, tiled=True)  23.4 us
    all_to_all x1, waiting for transfers between devices, local(): lax.all_to_all(densities, 'tm', split_axis=3, concat_axis=0, tiled=True)  7.58 us
    all_to_all x1, starting transfers between devices, local(): lax.all_to_all(densities, 'tm', split_axis=3, concat_axis=0, tiled=True)  5.83 us
    all_gather x1, local copies, waits for them, and re-layouts, local(): block_coords = lax.all_gather(positions, 'wave', axis=2, tiled=True)  3.35 us
  transfers between devices with their start and end apart: 2, of which 2 were waited for; matrix products, arithmetic and copies ran while one was open for 1% of the time, Pallas kernels for 0%

profile of v2, /device:TPU:8, one launch (start us, length us, event | category | flops | bytes accessed | tf_op | source)
XLA Modules:
  0.0 162.0 jit_solution(12064307954441787326)
XLA Ops:
  7.2 0.8 copy.19
  8.1 54.2 %all_gather.3 = f32[16,3,2048]{0,1,2:T(4,128)} all-gather(f32[16,3,64]{0,1,2:T(4,128)S(1)} %copy.19), channel_id=1, replica_groups=mesh['atom'=4,'tm'=4,'wave'=32] {'wave'}, dimensions={2}, use_global_device_ids=true | all-gather | bytes 405504 | tf_op jit(solution)/shard_map/all_gather | solution.py:158
  62.3 3.3 %copy.21 = f32[16,3,2048]{2,0,1:T(8,128)S(1)} copy(f32[16,3,2048]{0,1,2:T(4,128)} %all_gather.3) | data formatting | bytes 786432 | tf_op jit(solution)/shard_map/all_gather | solution.py:158
  65.7 1.5 cosine_bitcast_fusion
  67.2 1.4 copy.23.base_ref
  68.8 0.7 add_convert_fusion.3.pick_x_ref
  69.4 0.1 iota_compare_fusion
  69.5 0.7 add_convert_fusion.pick_y_ref
  70.3 0.7 add_convert_fusion.1.pick_z_ref
  71.0 0.6 add_convert_fusion.2.onehot_ref
  71.6 38.6 %shard_map.59 = f32[16,2,2,16,128]{4,3,2,1,0:T(8,128)} custom-call(f32[16,6,2048]{2,1,0:T(8,128)} %copy.23.base_ref, f32[2,2048]{1,0:T(2,128)} %add_convert_fusion.2.onehot_ref, bf16[16,32]{1,0:T(8,128)(2,1)} %add_convert_fusion.3.pick_x_ref, bf16[128,96]{1,0:T(8,128)(2,1)} %add_convert_fusion.pick_y_ref, bf16[128,96]{1,0:T(8,128)(2,1)} %add_convert_fusion.1.pick_z_ref), custom_call_target="tpu_custom_call" | custom-call | tf_op jit(solution)/shard_map/pallas_call | solution.py:166
  110.2 2.1 %copy.24 = f32[16,2,2,16,128]{4,0,2,1,3:T(8,128)} copy(f32[16,2,2,16,128]{4,3,2,1,0:T(8,128)} %shard_map.59) | data formatting | bytes 1048576 | tf_op jit(solution)/shard_map/pallas_call | solution.py:166
  112.4 23.4 %reduce-scatter.2.cloned.1.call-done = f32[16,2,2,4,128]{4,0,2,1,3:T(8,128)} async-done(((f32[16,2,2,16,128]{4,0,2,1,3:T(8,128)}), f32[16,2,2,4,128]{4,0,2,1,3:T(8,128)}) %reduce-scatter.2.cloned.1.call-update) | async-done | bytes 131088 | tf_op jit(solution)/shard_map/reduce_scatter | solution.py:185
  135.8 0.9 broadcast_multiply_fusion.1
  136.7 0.7 copy.25
  137.4 5.8 %all-to-all-start = ((f32[16,2,2,4,128]{4,2,1,0,3:T(2,128)}), f32[16,2,2,4,128]{4,2,1,0,3:T(2,128)S(1)}, u32[]{:S(2)}, u32[]{:S(2)}) async-start(f32[16,2,2,4,128]{4,2,1,0,3:T(2,128)} %copy.25), calls=%async_computation.1 | async-start | bytes 262144 | tf_op jit(solution)/shard_map/all_to_all | solution.py:187
  143.3 0.7 multiply_reduce_fusion
  144.0 0.7 copy.32
  144.8 7.6 %all-to-all-done = f32[16,2,2,4,128]{4,2,1,0,3:T(2,128)S(1)} async-done(((f32[16,2,2,4,128]{4,2,1,0,3:T(2,128)}), f32[16,2,2,4,128]{4,2,1,0,3:T(2,128)S(1)}, u32[]{:S(2)}, u32[]{:S(2)}) %all-to-all-start) | async-done | bytes 131104 | tf_op jit(solution)/shard_map/all_to_all | solution.py:187
  152.4 0.3 fusion.3
  152.8 0.3 fusion.2
  153.1 0.3 fusion
  153.5 0.3 convolution_add_fusion
  153.8 1.3 maximum_divide_fusion
  (20 shorter events, 0.4 us)
Async XLA Ops:
  7.2 128.6 %reduce-scatter.2.cloned.1.call-start = ((), (), s32[]{:S(2)}) async-start(), calls=%async_computation.2 | async-start | bytes 655360 | tf_op jit(solution)/shard_map/reduce_scatter | solution.py:185
  62.3 6.3 %copy-start = (s32[2048]{0:T(1024)S(1)}, s32[2048]{0:T(1024)}, u32[]{:S(2)}) copy-start(s32[2048]{0:T(1024)} %param.5) | copy-start | bytes 24580
  62.3 6.4 %copy-start.2 = (s32[16]{0:T(128)S(1)}, s32[16]{0:T(128)}, u32[]{:S(2)}) copy-start(s32[16]{0:T(128)} %param.6) | copy-start | bytes 196
  62.3 7.1 %copy-start.1 = (s32[2,128]{1,0:T(2,128)S(1)}, s32[2,128]{1,0:T(2,128)}, u32[]{:S(2)}) copy-start(s32[2,128]{1,0:T(2,128)} %param.7) | copy-start | bytes 3076
  137.4 14.9 %all-to-all-start = ((f32[16,2,2,4,128]{4,2,1,0,3:T(2,128)}), f32[16,2,2,4,128]{4,2,1,0,3:T(2,128)S(1)}, u32[]{:S(2)}, u32[]{:S(2)}) async-start(f32[16,2,2,4,128]{4,2,1,0,3:T(2,128)} %copy.25), calls=%async_computation.1 | async-start | bytes 262144 | tf_op jit(solution)/shard_map/all_to_all | solution.py:187
Sparse Core Ops, SparseCore 0:
  112.5 23.2 reduce-scatter.1

commit v3 on v2

--- a/solution.py
+++ b/solution.py
@@ -155,7 +155,7 @@
     kyz_local = kyz_index.shape[1]
     total_atoms = positions.shape[2] * lax.axis_size("atom") * lax.axis_size("wave")
     onehot_all = jnp.stack([species == 0, species == 1]).astype(jnp.float32)
-    block_coords = lax.all_gather(positions, "wave", axis=2, tiled=True)
+    block_coords = gathered_copies(positions, "wave", 2)
     atom_count = block_coords.shape[2]
     angle = TWO_PI * frac_turns(block_coords)
     base = jnp.stack([jnp.cos(angle), jnp.sin(angle)], axis=2).reshape(local_frames, 6, atom_count)
@@ -182,7 +182,7 @@
             pltpu.VMEM((2, 32, atom_count), jnp.bfloat16),
         ],
     )(base, onehot_all, pick_x, pick_y, pick_z)
-    owned = lax.psum_scatter(partial_value, "atom", scatter_dimension=3, tiled=True)
+    owned = sent_and_summed(partial_value, "atom", 3)
     densities = owned / jnp.sqrt(jnp.float32(total_atoms))
     spectra = transform(lax.all_to_all(densities, "tm", split_axis=3, concat_axis=0, tiled=True))
     return (spectra, densities)

time: 162 us -> 106 us (0.65)
  blocking collectives: 54.2 us -> 13.4 us
  waiting for transfers between devices: 31 us -> 16.9 us
  between operations: 14.2 us -> 0.83 us
  starting transfers between devices: 5.87 us -> 18.3 us
    all_gather x1 -> x0, blocking collectives: 54.2 us -> none  [local(): block_coords = lax.all_gather(positions, 'wave', axis=2, tiled=True)]
    reduce_scatter x1 -> x0, waiting for transfers between devices: 23.4 us -> none  [local(): lax.psum_scatter(partial_value, 'atom', scatter_dimension=3, tiled=True)]
    all_to_all x0 -> x1, blocking collectives: none -> 13.4 us  [sent_and_summed(): lax.all_to_all(pieces, axis, split_axis=0, concat_axis=0, tiled=True)]
    all_to_all x0 -> x1, starting transfers between devices: none -> 12.1 us  [copy_for_each(): lax.all_to_all(jnp.broadcast_to(shard[None], (peers, *shard.shape)), axis...]
    all_to_all x0 -> x1, waiting for transfers between devices: none -> 9.23 us  [copy_for_each(): lax.all_to_all(jnp.broadcast_to(shard[None], (peers, *shard.shape)), axis...]
    all_gather x1 -> x0, local copies, waits for them, and re-layouts: 3.35 us -> none  [local(): block_coords = lax.all_gather(positions, 'wave', axis=2, tiled=True)]
    pallas_call x1 -> x0, local copies, waits for them, and re-layouts: 2.14 us -> none  [local(): pl.pallas_call(frame_kernel, grid=(local_frames,), in_specs=[pl.BlockSpec...]
    unnamed x8 -> x13, local copies, waits for them, and re-layouts: 1.6 us -> 3.46 us
  transfers between devices with their start and end apart: 2 -> 2, of which waited for: 2 -> 2; matrix products, arithmetic and copies ran while one was open for 1% -> 3% of each run, Pallas kernels for 0% -> 0%
where the time goes in v3:
time: 106 us; the launch traced here: 105 us
  Pallas kernels  38.6 us (36%)
  starting transfers between devices  18.3 us (17%)
  waiting for transfers between devices  16.9 us (16%)
  blocking collectives  13.4 us (13%)
  other arithmetic  8.05 us (8%)
  local copies, waits for them, and re-layouts  7.88 us (7%)
  matrix products  1.33 us (1%)
    pallas_call x1, Pallas kernels, local(): pl.pallas_call(frame_kernel, grid=(local_frames,), in_specs=[pl.BlockSpec...  38.6 us
    all_to_all x1, blocking collectives, sent_and_summed(): lax.all_to_all(pieces, axis, split_axis=0, concat_axis=0, tiled=True)  13.4 us
    all_to_all x1, starting transfers between devices, copy_for_each(): lax.all_to_all(jnp.broadcast_to(shard[None], (peers, *shard.shape)), axis...  12.1 us
    all_to_all x1, waiting for transfers between devices, copy_for_each(): lax.all_to_all(jnp.broadcast_to(shard[None], (peers, *shard.shape)), axis...  9.23 us
    all_to_all x1, waiting for transfers between devices, local(): lax.all_to_all(densities, 'tm', split_axis=3, concat_axis=0, tiled=True)  7.68 us
    all_to_all x1, starting transfers between devices, local(): lax.all_to_all(densities, 'tm', split_axis=3, concat_axis=0, tiled=True)  6.21 us
    unnamed x13, local copies, waits for them, and re-layouts  3.46 us
  transfers between devices with their start and end apart: 2, of which 2 were waited for; matrix products, arithmetic and copies ran while one was open for 3% of the time, Pallas kernels for 0%

profile of v3, /device:TPU:8, one launch (start us, length us, event | category | flops | bytes accessed | tf_op | source)
XLA Modules:
  0.0 105.3 jit_solution(9892873115291382688)
XLA Ops:
  0.6 0.7 copy-done
  1.4 1.2 %reshape.321 = f32[32,1,3072]{2,1,0:T(1,128)} reshape(f32[32,3,16,64]{3,2,1,0:T(8,128)S(1)} %broadcast_bitcast_fusion) | data formatting | bytes 786432
  2.7 12.1 %all-to-all-start = ((f32[32,1,3072]{2,1,0:T(1,128)}), f32[32,1,3072]{2,1,0:T(1,128)S(1)}, u32[]{:S(2)}, u32[]{:S(2)}) async-start(f32[32,1,3072]{2,1,0:T(1,128)} %reshape.321), calls=%async_computation | async-start | bytes 786432 | tf_op jit(solution)/shard_map/all_to_all | solution.py:15
  14.8 0.6 copy-done.4
  15.5 0.6 copy-done.3
  16.1 0.7 add_convert_fusion.3.pick_x_ref
  16.9 0.7 add_convert_fusion.pick_y_ref
  17.6 0.7 add_convert_fusion.1.pick_z_ref
  18.3 0.6 add_convert_fusion.2.onehot_ref
  18.9 9.2 %all-to-all-done = f32[32,1,3072]{2,1,0:T(1,128)S(1)} async-done(((f32[32,1,3072]{2,1,0:T(1,128)}), f32[32,1,3072]{2,1,0:T(1,128)S(1)}, u32[]{:S(2)}, u32[]{:S(2)}) %all-to-all-start) | async-done | bytes 393248 | tf_op jit(solution)/shard_map/all_to_all | solution.py:15
  28.2 0.5 broadcast.106
  28.7 1.5 %reduce = f32[32,3072]{1,0:T(8,128)S(1)} reduce(f32[32,1,3072]{2,1,0:T(1,128)S(1)} %all-to-all-done, f32[]{:T(128)} %broadcast.106), dimensions={1}, to_apply=%all_to_all.19.reduce_sub_computation | reduce | bytes 786436 | tf_op jit(solution)/shard_map/all_to_all | solution.py:15
  31.0 1.5 %fusion.3 = (f32[16,3,1,2048]{3,0,2,1:T(8,128)S(1)}, f32[16,3,1,2048]{3,0,2,1:T(8,128)S(1)}) fusion(f32[16,3,1,2048]{3,0,2,1:T(8,128)S(1)} %reshape.314), kind=kLoop, calls=%fused_computation.8 | loop fusion | flops 294912 | bytes 1179648 | tf_op jit(solution)/shard_map/cos | solution.py:161
  32.5 1.4 %copy.28.base_ref = f32[16,6,2048]{2,1,0:T(8,128)} copy(f32[16,6,2048]{2,0,1:T(8,128)S(1)} %bitcast.63) | data formatting | bytes 1572864 | tf_op jit(solution)/shard_map/reshape | solution.py:161
  34.0 38.6 %shard_map.59 = f32[16,2,2,16,128]{4,3,2,1,0:T(8,128)} custom-call(f32[16,6,2048]{2,1,0:T(8,128)} %copy.28.base_ref, f32[2,2048]{1,0:T(2,128)} %add_convert_fusion.2.onehot_ref, bf16[16,32]{1,0:T(8,128)(2,1)} %add_convert_fusion.3.pick_x_ref, bf16[128,96]{1,0:T(8,128)(2,1)} %add_convert_fusion.pick_y_ref, bf16[128,96]{1,0:T(8,128)(2,1)} %add_convert_fusion.1.pick_z_ref), custom_call_target="tpu_custom_call" | custom-call | tf_op jit(solution)/shard_map/pallas_call | solution.py:166
  72.6 1.1 %copy.37 = f32[16,2,2,4,4,128]{5,4,2,1,0,3:T(4,128)S(1)} copy(f32[16,2,2,4,4,128]{5,4,3,2,1,0:T(4,128)} %bitcast.64) | data formatting | bytes 1048576 | tf_op jit(solution)/shard_map/reshape | solution.py:33
  73.7 13.4 %all_to_all.28 = f32[4,16,2,2,4,128]{5,4,3,2,1,0:T(4,128)S(1)} all-to-all(f32[4,16,2,2,4,128]{5,4,3,2,1,0:T(4,128)S(1)} %bitcast.65), channel_id=1, replica_groups=mesh['atom'=4,'tm'=4,'wave'=32] {'atom'}, dimensions={0} | all-to-all | bytes 1048576 | tf_op jit(solution)/shard_map/all_to_all | solution.py:39
  87.3 0.7 copy.30
  88.0 6.2 %all-to-all-start.2 = ((f32[16,2,2,4,128]{4,0,2,1,3:T(8,128)}), f32[16,2,2,4,128]{4,0,2,1,3:T(8,128)S(1)}, u32[]{:S(2)}, u32[]{:S(2)}) async-start(f32[16,2,2,4,128]{4,0,2,1,3:T(8,128)} %copy.30), calls=%async_computation.2 | async-start | bytes 262144 | tf_op jit(solution)/shard_map/all_to_all | solution.py:187
  94.2 0.7 multiply_reduce_fusion
  94.9 7.7 %all-to-all-done.2 = f32[16,2,2,4,128]{4,0,2,1,3:T(8,128)S(1)} async-done(((f32[16,2,2,4,128]{4,0,2,1,3:T(8,128)}), f32[16,2,2,4,128]{4,0,2,1,3:T(8,128)S(1)}, u32[]{:S(2)}, u32[]{:S(2)}) %all-to-all-start.2) | async-done | bytes 131104 | tf_op jit(solution)/shard_map/all_to_all | solution.py:187
  103.4 0.3 fusion
  103.7 0.3 convolution_add_fusion
  104.1 1.2 %maximum_divide_fusion = f32[3,64,1,128]{3,1,2,0:T(8,128)} fusion(f32[1,64,1,128]{3,1,2,0:T(8,128)S(1)} %fusion.9, f32[1,64,1,128]{3,1,2,0:T(8,128)S(1)} %get-tuple-element.13, f32[1,64,1,128]{3,1,2,0:T(8,128)S(1)} %get-tuple-element.12, f32[]{:T(128)} %multiply_reduce_fusion), kind=kLoop, calls=%fused_computation.9 | loop fusion | flops 73728 | bytes 196612 | tf_op jit(solution)/shard_map/div | solution.py:80
  (29 shorter events, 2.1 us)
Async XLA Ops:
  0.6 0.7 copy-start
  2.7 12.1 %copy-start.2 = (s32[2048]{0:T(1024)S(1)}, s32[2048]{0:T(1024)}, u32[]{:S(2)}) copy-start(s32[2048]{0:T(1024)} %param.5) | copy-start | bytes 24580
  2.7 25.5 %all-to-all-start = ((f32[32,1,3072]{2,1,0:T(1,128)}), f32[32,1,3072]{2,1,0:T(1,128)S(1)}, u32[]{:S(2)}, u32[]{:S(2)}) async-start(f32[32,1,3072]{2,1,0:T(1,128)} %reshape.321), calls=%async_computation | async-start | bytes 786432 | tf_op jit(solution)/shard_map/all_to_all | solution.py:15
  14.8 0.7 copy-start.4
  15.4 0.7 copy-start.3
  87.3 0.7 copy-start.1
  88.0 14.6 %all-to-all-start.2 = ((f32[16,2,2,4,128]{4,0,2,1,3:T(8,128)}), f32[16,2,2,4,128]{4,0,2,1,3:T(8,128)S(1)}, u32[]{:S(2)}, u32[]{:S(2)}) async-start(f32[16,2,2,4,128]{4,0,2,1,3:T(8,128)} %copy.30), calls=%async_computation.2 | async-start | bytes 262144 | tf_op jit(solution)/shard_map/all_to_all | solution.py:187

commit v4 on v3

--- a/solution.py
+++ b/solution.py
@@ -55,13 +55,14 @@
     return jnp.stack([real_part, imag_part], axis=1)
 
 
-def transform(series):
+def transform(series, frame_of_row):
     length = series.shape[0]
-    window = hann_window(length)
-    energy = jnp.sum(window * window)
+    energy_window = hann_window(length)
+    energy = jnp.sum(energy_window * energy_window)
+    window = 0.5 - 0.5 * jnp.cos(TWO_PI / length * (frame_of_row.astype(jnp.float32) + 0.5))
     weighted = series * window[:, None, None, None, None]
     frame_steps = jnp.arange(length)
-    phase_turns = (frame_steps[:, None] * frame_steps[None, :] % length).astype(jnp.float32)
+    phase_turns = (frame_steps[:, None] * frame_of_row[None, :] % length).astype(jnp.float32)
     dft_angle = TWO_PI / length * phase_turns
     cos_table = jnp.cos(dft_angle)
     sin_table = jnp.sin(dft_angle)
@@ -78,6 +79,17 @@
     cross_pair = spec_real[:, 0] * spec_real[:, 1] + spec_imag[:, 0] * spec_imag[:, 1]
     hydrogen_pair = spec_real[:, 1] * spec_real[:, 1] + spec_imag[:, 1] * spec_imag[:, 1]
     return jnp.stack([oxygen_pair, cross_pair, hydrogen_pair]) / energy
+
+
+def shifted_blocks(blocks, axis):
+    peers = lax.axis_size(axis)
+    me = lax.axis_index(axis)
+    arrived = [lax.dynamic_index_in_dim(blocks, me, 0, keepdims=False)]
+    for shift in range(1, peers):
+        outgoing = lax.dynamic_index_in_dim(blocks, (me + shift) % peers, 0, keepdims=False)
+        pairs = [(src, (src + shift) % peers) for src in range(peers)]
+        arrived.append(lax.ppermute(outgoing, axis, pairs))
+    return arrived
 
 
 def power_rows(base_cos, base_sin, count):
@@ -182,9 +194,18 @@
             pltpu.VMEM((2, 32, atom_count), jnp.bfloat16),
         ],
     )(base, onehot_all, pick_x, pick_y, pick_z)
-    owned = sent_and_summed(partial_value, "atom", 3)
+    atom_peers = lax.axis_size("atom")
+    time_peers = lax.axis_size("tm")
+    owned_parts = shifted_blocks(cut_along(partial_value, 3, atom_peers), "atom")
+    owned = owned_parts[0]
+    for part in owned_parts[1:]:
+        owned = owned + part
     densities = owned / jnp.sqrt(jnp.float32(total_atoms))
-    spectra = transform(lax.all_to_all(densities, "tm", split_axis=3, concat_axis=0, tiled=True))
+    series = jnp.concatenate(shifted_blocks(cut_along(densities, 3, time_peers), "tm"), axis=0)
+    me = lax.axis_index("tm")
+    sources = (me - jnp.arange(time_peers)) % time_peers
+    frame_of_row = (sources[:, None] * local_frames + jnp.arange(local_frames)[None, :]).reshape(-1)
+    spectra = transform(series, frame_of_row)
     return (spectra, densities)
 
 

time: 106 us -> 111 us (1.047)
  starting transfers between devices: 18.3 us -> 35.7 us
  blocking collectives: 13.4 us -> 0 us
    ppermute x0 -> x6, starting transfers between devices: none -> 23.7 us  [shifted_blocks(): arrived.append(lax.ppermute(outgoing, axis, pairs))]
    all_to_all x1 -> x0, blocking collectives: 13.4 us -> none  [sent_and_summed(): lax.all_to_all(pieces, axis, split_axis=0, concat_axis=0, tiled=True)]
    ppermute x0 -> x6, waiting for transfers between devices: none -> 8.62 us  [shifted_blocks(): arrived.append(lax.ppermute(outgoing, axis, pairs))]
    all_to_all x1 -> x0, waiting for transfers between devices: 7.68 us -> none  [local(): lax.all_to_all(densities, 'tm', split_axis=3, concat_axis=0, tiled=True)]
    all_to_all x1 -> x0, starting transfers between devices: 6.21 us -> none  [local(): lax.all_to_all(densities, 'tm', split_axis=3, concat_axis=0, tiled=True)]
    another operation x0 -> x4, local copies, waits for them, and re-layouts: none -> 1.28 us
    reshape x1 -> x0, local copies, waits for them, and re-layouts: 1.14 us -> none  [cut_along(): shard.reshape(*dims[:dim], peers, dims[dim] // peers, *dims[dim + 1:])]
    unnamed x13 -> x12, local copies, waits for them, and re-layouts: 3.46 us -> 4.28 us
  transfers between devices with their start and end apart: 2 -> 7, of which waited for: 2 -> 4; matrix products, arithmetic and copies ran while one was open for 3% -> 4% of each run, Pallas kernels for 0% -> 0%
where the time goes in v4:
time: 111 us
  Pallas kernels  38.6 us (35%)
  starting transfers between devices  35.7 us (32%)
  waiting for transfers between devices  17.7 us (16%)
  local copies, waits for them, and re-layouts  8.25 us (7%)
  other arithmetic  8.07 us (7%)
  matrix products  1.33 us (1%)
    pallas_call x1, Pallas kernels, local(): pl.pallas_call(frame_kernel, grid=(local_frames,), in_specs=[pl.BlockSpec...  38.6 us
    ppermute x6, starting transfers between devices, shifted_blocks(): arrived.append(lax.ppermute(outgoing, axis, pairs))  23.7 us
    all_to_all x1, starting transfers between devices, copy_for_each(): lax.all_to_all(jnp.broadcast_to(shard[None], (peers, *shard.shape)), axis...  11.9 us
    all_to_all x1, waiting for transfers between devices, copy_for_each(): lax.all_to_all(jnp.broadcast_to(shard[None], (peers, *shard.shape)), axis...  9.06 us
    ppermute x6, waiting for transfers between devices, shifted_blocks(): arrived.append(lax.ppermute(outgoing, axis, pairs))  8.62 us
    unnamed x12, local copies, waits for them, and re-layouts  4.28 us
  transfers between devices with their start and end apart: 7, of which 4 were waited for; matrix products, arithmetic and copies ran while one was open for 4% of the time, Pallas kernels for 0%

profile of v4, /device:TPU:8, one launch (start us, length us, event | category | flops | bytes accessed | tf_op | source)
XLA Modules:
  0.0 110.6 jit_solution(1108503480461723689)
XLA Ops:
  0.6 0.7 copy-done
  1.4 1.2 %reshape.427 = f32[32,1,3072]{2,1,0:T(1,128)} reshape(f32[32,3,16,64]{3,2,1,0:T(8,128)S(1)} %broadcast_bitcast_fusion) | data formatting | bytes 786432
  2.7 11.9 %all-to-all-start = ((f32[32,1,3072]{2,1,0:T(1,128)}), f32[32,1,3072]{2,1,0:T(1,128)S(1)}, u32[]{:S(2)}, u32[]{:S(2)}) async-start(f32[32,1,3072]{2,1,0:T(1,128)} %reshape.427), calls=%async_computation | async-start | bytes 786432 | tf_op jit(solution)/shard_map/all_to_all | solution.py:15
  14.7 0.7 copy-done.1
  16.1 0.7 add_convert_fusion.3.pick_x_ref
  16.9 0.7 add_convert_fusion.pick_y_ref
  17.6 0.7 add_convert_fusion.1.pick_z_ref
  19.0 9.1 %all-to-all-done = f32[32,1,3072]{2,1,0:T(1,128)S(1)} async-done(((f32[32,1,3072]{2,1,0:T(1,128)}), f32[32,1,3072]{2,1,0:T(1,128)S(1)}, u32[]{:S(2)}, u32[]{:S(2)}) %all-to-all-start) | async-done | bytes 393248 | tf_op jit(solution)/shard_map/all_to_all | solution.py:15
  28.6 1.5 %reduce = f32[32,3072]{1,0:T(8,128)S(1)} reduce(f32[32,1,3072]{2,1,0:T(1,128)S(1)} %all-to-all-done, f32[]{:T(128)} %broadcast.164), dimensions={1}, to_apply=%all_to_all.3.reduce_sub_computation | reduce | bytes 786436 | tf_op jit(solution)/shard_map/all_to_all | solution.py:15
  30.9 1.5 %fusion.3 = (f32[16,3,1,2048]{3,0,2,1:T(8,128)S(1)}, f32[16,3,1,2048]{3,0,2,1:T(8,128)S(1)}) fusion(f32[16,3,1,2048]{3,0,2,1:T(8,128)S(1)} %reshape.420), kind=kLoop, calls=%fused_computation.7 | loop fusion | flops 294912 | bytes 1179648 | tf_op jit(solution)/shard_map/cos | solution.py:173
  32.4 1.4 %copy.27.base_ref = f32[16,6,2048]{2,1,0:T(8,128)} copy(f32[16,6,2048]{2,0,1:T(8,128)S(1)} %bitcast.73) | data formatting | bytes 1572864 | tf_op jit(solution)/shard_map/reshape | solution.py:173
  33.9 38.6 %shard_map.59 = f32[16,2,2,16,128]{4,3,2,1,0:T(8,128)} custom-call(f32[16,6,2048]{2,1,0:T(8,128)} %copy.27.base_ref, f32[2,2048]{1,0:T(2,128)} %add_convert_fusion.2.onehot_ref, bf16[16,32]{1,0:T(8,128)(2,1)} %add_convert_fusion.3.pick_x_ref, bf16[128,96]{1,0:T(8,128)(2,1)} %add_convert_fusion.pick_y_ref, bf16[128,96]{1,0:T(8,128)(2,1)} %add_convert_fusion.1.pick_z_ref), custom_call_target="tpu_custom_call" | custom-call | tf_op jit(solution)/shard_map/pallas_call | solution.py:178
  72.5 1.1 %constant_dynamic-slice_fusion.7 = (f32[16,2,2,1,4,128]{5,4,3,2,1,0:T(4,128)S(1)}, f32[16,2,2,1,4,128]{5,4,3,2,1,0:T(4,128)S(1)}, f32[16,2,2,1,4,128]{5,4,3,2,1,0:T(4,128)S(1)}, f32[16,2,2,1,4,128]{5,4,3,2,1,0:T(4,128)S(1)}) fusion(f32[16,2,2,4,4,128]{5,4,3,2,1,0:T(4,128)} %bitcast.74, s32[]{:T(128)S(6)} %select_n.71, s32[]{:T(128)S(6)} %select_n.77, ...), kind=kLoop, calls=%fused_computation.64 | loop fusion | bytes 1048592 | tf_op jit(solution)/shard_map/dynamic-slice
  73.7 4.7 %collective-permute-start.2 = (f32[16,2,2,4,128]{4,0,1,3,2:T(8,128)S(1)}, f32[16,2,2,4,128]{4,0,1,3,2:T(8,128)S(1)}, u32[]{:S(2)}, u32[]{:S(2)}) collective-permute-start(f32[16,2,2,4,128]{4,0,1,3,2:T(8,128)S(1)} %bitcast.78), channel_id=1, source_target_pairs={{0,384},{128,0},{256,128},{384,256},{1,385},{129,1},{257,129},{385... | collective-permute-start | bytes 393224 | tf_op jit(solution)/shard_map/ppermute | solution.py:91
  78.4 2.7 %collective-permute-start.1 = (f32[16,2,2,4,128]{4,0,1,3,2:T(8,128)S(1)}, f32[16,2,2,4,128]{4,0,1,3,2:T(8,128)S(1)}, u32[]{:S(2)}, u32[]{:S(2)}) collective-permute-start(f32[16,2,2,4,128]{4,0,1,3,2:T(8,128)S(1)} %bitcast.79), channel_id=1, source_target_pairs={{0,256},{128,384},{256,0},{384,128},{1,257},{129,385},{257,1},{385... | collective-permute-start | bytes 393224 | tf_op jit(solution)/shard_map/ppermute | solution.py:91
  81.2 2.8 %collective-permute-start = (f32[16,2,2,4,128]{4,0,1,3,2:T(8,128)S(1)}, f32[16,2,2,4,128]{4,0,1,3,2:T(8,128)S(1)}, u32[]{:S(2)}, u32[]{:S(2)}) collective-permute-start(f32[16,2,2,4,128]{4,0,1,3,2:T(8,128)S(1)} %bitcast.80), channel_id=1, source_target_pairs={{0,128},{128,256},{256,384},{384,0},{1,129},{129,257},{257,385},{3... | collective-permute-start | bytes 393224 | tf_op jit(solution)/shard_map/ppermute | solution.py:91
  84.1 3.6 %collective-permute-done.1 = f32[16,2,2,4,128]{4,0,1,3,2:T(8,128)S(1)} collective-permute-done((f32[16,2,2,4,128]{4,0,1,3,2:T(8,128)S(1)}, f32[16,2,2,4,128]{4,0,1,3,2:T(8,128)S(1)}, u32[]{:S(2)}, u32[]{:S(2)}) %collective-permute-start.1) | collective-permute-done | bytes 131104 | tf_op jit(solution)/shard_map/ppermute | solution.py:91
  87.8 1.9 %collective-permute-done = f32[16,2,2,4,128]{4,0,1,3,2:T(8,128)S(1)} collective-permute-done((f32[16,2,2,4,128]{4,0,1,3,2:T(8,128)S(1)}, f32[16,2,2,4,128]{4,0,1,3,2:T(8,128)S(1)}, u32[]{:S(2)}, u32[]{:S(2)}) %collective-permute-start) | collective-permute-done | bytes 131104 | tf_op jit(solution)/shard_map/ppermute | solution.py:91
  89.8 5.3 %collective-permute-start.5 = (f32[16,2,2,1,128]{4,0,1,3,2:T(8,128)S(1)}, f32[16,2,2,1,128]{4,0,1,3,2:T(8,128)S(1)}, u32[]{:S(2)}, u32[]{:S(2)}) collective-permute-start(f32[16,2,2,1,128]{4,0,1,3,2:T(8,128)S(1)} %get-tuple-element.17), channel_id=1, source_target_pairs={{0,96},{32,0},{64,32},{96,64},{1,97},{33,1},{65,33},{97,65},{2,98}... | collective-permute-start | bytes 98312 | tf_op jit(solution)/shard_map/ppermute | solution.py:91
  95.0 4.7 %collective-permute-start.4 = (f32[16,2,2,1,128]{4,0,1,3,2:T(8,128)S(1)}, f32[16,2,2,1,128]{4,0,1,3,2:T(8,128)S(1)}, u32[]{:S(2)}, u32[]{:S(2)}) collective-permute-start(f32[16,2,2,1,128]{4,0,1,3,2:T(8,128)S(1)} %get-tuple-element.18), channel_id=1, source_target_pairs={{0,64},{32,96},{64,0},{96,32},{1,65},{33,97},{65,1},{97,33},{2,66}... | collective-permute-start | bytes 98312 | tf_op jit(solution)/shard_map/ppermute | solution.py:91
  99.8 3.6 %collective-permute-start.3 = (f32[16,2,2,1,128]{4,0,1,3,2:T(8,128)S(1)}, f32[16,2,2,1,128]{4,0,1,3,2:T(8,128)S(1)}, u32[]{:S(2)}, u32[]{:S(2)}) collective-permute-start(f32[16,2,2,1,128]{4,0,1,3,2:T(8,128)S(1)} %get-tuple-element.19), channel_id=1, source_target_pairs={{0,32},{32,64},{64,96},{96,0},{1,33},{33,65},{65,97},{97,1},{2,34}... | collective-permute-start | bytes 98312 | tf_op jit(solution)/shard_map/ppermute | solution.py:91
  104.1 0.7 copy.36
  104.8 3.1 %collective-permute-done.3 = f32[16,2,2,1,128]{4,0,1,3,2:T(8,128)S(1)} collective-permute-done((f32[16,2,2,1,128]{4,0,1,3,2:T(8,128)S(1)}, f32[16,2,2,1,128]{4,0,1,3,2:T(8,128)S(1)}, u32[]{:S(2)}, u32[]{:S(2)}) %collective-permute-start.3) | collective-permute-done | bytes 32800 | tf_op jit(solution)/shard_map/ppermute | solution.py:91
  109.4 1.2 %maximum_divide_fusion = f32[3,64,1,128]{3,1,2,0:T(8,128)} fusion(f32[1,64,1,128]{3,1,2,0:T(8,128)S(1)} %fusion.12, f32[1,64,1,128]{3,1,2,0:T(8,128)S(1)} %get-tuple-element.15, f32[1,64,1,128]{3,1,2,0:T(8,128)S(1)} %get-tuple-element.14, f32[]{:T(128)} %multiply_reduce_fusion), kind=kLoop, calls=%fused_computation.16 | loop fusion | flops 73728 | bytes 196612 | tf_op jit(solution)/shard_map/div | solution.py:81
  (41 shorter events, 5.4 us)
Async XLA Ops:
  0.6 0.7 copy-start
  2.7 25.4 %all-to-all-start = ((f32[32,1,3072]{2,1,0:T(1,128)}), f32[32,1,3072]{2,1,0:T(1,128)S(1)}, u32[]{:S(2)}, u32[]{:S(2)}) async-start(f32[32,1,3072]{2,1,0:T(1,128)} %reshape.427), calls=%async_computation | async-start | bytes 786432 | tf_op jit(solution)/shard_map/all_to_all | solution.py:15
  14.7 0.7 copy-start.1
  15.4 0.7 copy-start.3
  16.1 0.7 copy-start.2
  73.7 10.5 %collective-permute-start.2 = (f32[16,2,2,4,128]{4,0,1,3,2:T(8,128)S(1)}, f32[16,2,2,4,128]{4,0,1,3,2:T(8,128)S(1)}, u32[]{:S(2)}, u32[]{:S(2)}) collective-permute-start(f32[16,2,2,4,128]{4,0,1,3,2:T(8,128)S(1)} %bitcast.78), channel_id=1, source_target_pairs={{0,384},{128,0},{256,128},{384,256},{1,385},{129,1},{257,129},{385... | collective-permute-start | bytes 393224 | tf_op jit(solution)/shard_map/ppermute | solution.py:91
  78.4 9.4 %collective-permute-start.1 = (f32[16,2,2,4,128]{4,0,1,3,2:T(8,128)S(1)}, f32[16,2,2,4,128]{4,0,1,3,2:T(8,128)S(1)}, u32[]{:S(2)}, u32[]{:S(2)}) collective-permute-start(f32[16,2,2,4,128]{4,0,1,3,2:T(8,128)S(1)} %bitcast.79), channel_id=1, source_target_pairs={{0,256},{128,384},{256,0},{384,128},{1,257},{129,385},{257,1},{385... | collective-permute-start | bytes 393224 | tf_op jit(solution)/shard_map/ppermute | solution.py:91
  81.2 8.5 %collective-permute-start = (f32[16,2,2,4,128]{4,0,1,3,2:T(8,128)S(1)}, f32[16,2,2,4,128]{4,0,1,3,2:T(8,128)S(1)}, u32[]{:S(2)}, u32[]{:S(2)}) collective-permute-start(f32[16,2,2,4,128]{4,0,1,3,2:T(8,128)S(1)} %bitcast.80), channel_id=1, source_target_pairs={{0,128},{128,256},{256,384},{384,0},{1,129},{129,257},{257,385},{3... | collective-permute-start | bytes 393224 | tf_op jit(solution)/shard_map/ppermute | solution.py:91
  89.8 15.0 %collective-permute-start.5 = (f32[16,2,2,1,128]{4,0,1,3,2:T(8,128)S(1)}, f32[16,2,2,1,128]{4,0,1,3,2:T(8,128)S(1)}, u32[]{:S(2)}, u32[]{:S(2)}) collective-permute-start(f32[16,2,2,1,128]{4,0,1,3,2:T(8,128)S(1)} %get-tuple-element.17), channel_id=1, source_target_pairs={{0,96},{32,0},{64,32},{96,64},{1,97},{33,1},{65,33},{97,65},{2,98}... | collective-permute-start | bytes 98312 | tf_op jit(solution)/shard_map/ppermute | solution.py:91
  95.0 9.8 %collective-permute-start.4 = (f32[16,2,2,1,128]{4,0,1,3,2:T(8,128)S(1)}, f32[16,2,2,1,128]{4,0,1,3,2:T(8,128)S(1)}, u32[]{:S(2)}, u32[]{:S(2)}) collective-permute-start(f32[16,2,2,1,128]{4,0,1,3,2:T(8,128)S(1)} %get-tuple-element.18), channel_id=1, source_target_pairs={{0,64},{32,96},{64,0},{96,32},{1,65},{33,97},{65,1},{97,33},{2,66}... | collective-permute-start | bytes 98312 | tf_op jit(solution)/shard_map/ppermute | solution.py:91
  99.8 8.1 %collective-permute-start.3 = (f32[16,2,2,1,128]{4,0,1,3,2:T(8,128)S(1)}, f32[16,2,2,1,128]{4,0,1,3,2:T(8,128)S(1)}, u32[]{:S(2)}, u32[]{:S(2)}) collective-permute-start(f32[16,2,2,1,128]{4,0,1,3,2:T(8,128)S(1)} %get-tuple-element.19), channel_id=1, source_target_pairs={{0,32},{32,64},{64,96},{96,0},{1,33},{33,65},{65,97},{97,1},{2,34}... | collective-permute-start | bytes 98312 | tf_op jit(solution)/shard_map/ppermute | solution.py:91

commit v5 on v3

--- a/solution.py
+++ b/solution.py
@@ -97,8 +97,13 @@
     return lax.dot_general(picks, stacked[...], dims, preferred_element_type=jnp.float32)
 
 
-def frame_kernel(base_ref, onehot_ref, pick_x_ref, pick_y_ref, pick_z_ref, out_ref, axis_ref, x_ref, yz_half, x_half):
-    base = base_ref[0]
+def frame_kernel(base_ref, onehot_ref, pick_x_ref, pick_y_ref, pick_z_ref, out_ref, axis_all, x_all, yz_all, xh_all):
+  for f in range(base_ref.shape[0]):
+    axis_ref = axis_all.at[f]
+    x_ref = x_all.at[f]
+    yz_half = yz_all.at[f]
+    x_half = xh_all.at[f]
+    base = base_ref[f]
     kmax = 16
     rows_pad = axis_ref.shape[1]
     for axis in range(2):
@@ -139,8 +144,8 @@
     for s in range(2):
         cos_rows = slice((2 * s) * kx, (2 * s + 1) * kx)
         sin_rows = slice((2 * s + 1) * kx, (2 * s + 2) * kx)
-        out_ref[0, s, 0] = with_cos[cos_rows] - with_sin[sin_rows]
-        out_ref[0, s, 1] = -(with_sin[cos_rows] + with_cos[sin_rows])
+        out_ref[f, s, 0] = with_cos[cos_rows] - with_sin[sin_rows]
+        out_ref[f, s, 1] = -(with_sin[cos_rows] + with_cos[sin_rows])
 
 
 def picks_of(index, lowest, count):
@@ -160,26 +165,27 @@
     angle = TWO_PI * frac_turns(block_coords)
     base = jnp.stack([jnp.cos(angle), jnp.sin(angle)], axis=2).reshape(local_frames, 6, atom_count)
     rows_pad = 48
+    frames_per_step = math.gcd(local_frames, 4)
     pick_x = picks_of(kx_index, 1, 16)
     pick_y = picks_of(kyz_index[0], -16, rows_pad)
     pick_z = picks_of(kyz_index[1], -16, rows_pad)
     partial_value = pl.pallas_call(
         frame_kernel,
-        grid=(local_frames,),
+        grid=(local_frames // frames_per_step,),
         in_specs=[
-            pl.BlockSpec((1, 6, atom_count), lambda t: (t, 0, 0)),
+            pl.BlockSpec((frames_per_step, 6, atom_count), lambda t: (t, 0, 0)),
             pl.BlockSpec((2, atom_count), lambda t: (0, 0)),
             pl.BlockSpec((kx_count, 32), lambda t: (0, 0)),
             pl.BlockSpec((kyz_local, 2 * rows_pad), lambda t: (0, 0)),
             pl.BlockSpec((kyz_local, 2 * rows_pad), lambda t: (0, 0)),
         ],
-        out_specs=pl.BlockSpec((1, 2, 2, kx_count, kyz_local), lambda t: (t, 0, 0, 0, 0)),
+        out_specs=pl.BlockSpec((frames_per_step, 2, 2, kx_count, kyz_local), lambda t: (t, 0, 0, 0, 0)),
         out_shape=jax.ShapeDtypeStruct((local_frames, 2, 2, kx_count, kyz_local), jnp.float32),
         scratch_shapes=[
-            pltpu.VMEM((4, rows_pad, atom_count), jnp.float32),
-            pltpu.VMEM((2, 16, atom_count), jnp.float32),
-            pltpu.VMEM((4, 2 * rows_pad, atom_count), jnp.bfloat16),
-            pltpu.VMEM((2, 32, atom_count), jnp.bfloat16),
+            pltpu.VMEM((frames_per_step, 4, rows_pad, atom_count), jnp.float32),
+            pltpu.VMEM((frames_per_step, 2, 16, atom_count), jnp.float32),
+            pltpu.VMEM((frames_per_step, 4, 2 * rows_pad, atom_count), jnp.bfloat16),
+            pltpu.VMEM((frames_per_step, 2, 32, atom_count), jnp.bfloat16),
         ],
     )(base, onehot_all, pick_x, pick_y, pick_z)
     owned = sent_and_summed(partial_value, "atom", 3)

time: 106 us -> 97.8 us (0.923)
  Pallas kernels: 38.6 us -> 30.6 us
    pallas_call x1, Pallas kernels: 38.6 us -> 30.6 us  [local(): pl.pallas_call(frame_kernel, grid=(local_frames // frames_per_step,), in_...]
  transfers between devices with their start and end apart: 2 -> 2, of which waited for: 2 -> 2; matrix products, arithmetic and copies ran while one was open for 3% -> 4% of each run, Pallas kernels for 0% -> 0%
where the time goes in v5:
time: 97.8 us; the launch traced here: 97.3 us
  Pallas kernels  30.6 us (31%)
  starting transfers between devices  18.3 us (19%)
  waiting for transfers between devices  16.9 us (17%)
  blocking collectives  13.4 us (14%)
  other arithmetic  8.05 us (8%)
  local copies, waits for them, and re-layouts  7.88 us (8%)
  matrix products  1.33 us (1%)
    pallas_call x1, Pallas kernels, local(): pl.pallas_call(frame_kernel, grid=(local_frames // frames_per_step,), in_...  30.6 us
    all_to_all x1, blocking collectives, sent_and_summed(): lax.all_to_all(pieces, axis, split_axis=0, concat_axis=0, tiled=True)  13.4 us
    all_to_all x1, starting transfers between devices, copy_for_each(): lax.all_to_all(jnp.broadcast_to(shard[None], (peers, *shard.shape)), axis...  12.1 us
    all_to_all x1, waiting for transfers between devices, copy_for_each(): lax.all_to_all(jnp.broadcast_to(shard[None], (peers, *shard.shape)), axis...  9.23 us
    all_to_all x1, waiting for transfers between devices, local(): lax.all_to_all(densities, 'tm', split_axis=3, concat_axis=0, tiled=True)  7.68 us
    all_to_all x1, starting transfers between devices, local(): lax.all_to_all(densities, 'tm', split_axis=3, concat_axis=0, tiled=True)  6.2 us
    unnamed x13, local copies, waits for them, and re-layouts  3.46 us
    concatenate x3, other arithmetic, picks_of(): return jnp.concatenate([picks, picks], axis=1)  2.08 us
  transfers between devices with their start and end apart: 2, of which 2 were waited for; matrix products, arithmetic and copies ran while one was open for 4% of the time, Pallas kernels for 0%

profile of v5, /device:TPU:8, one launch (start us, length us, event | category | flops | bytes accessed | tf_op | source)
XLA Modules:
  0.0 97.3 jit_solution(6012861768851660018)
XLA Ops:
  0.6 0.7 copy-done
  1.4 1.2 %reshape.321 = f32[32,1,3072]{2,1,0:T(1,128)} reshape(f32[32,3,16,64]{3,2,1,0:T(8,128)S(1)} %broadcast_bitcast_fusion) | data formatting | bytes 786432
  2.7 12.1 %all-to-all-start = ((f32[32,1,3072]{2,1,0:T(1,128)}), f32[32,1,3072]{2,1,0:T(1,128)S(1)}, u32[]{:S(2)}, u32[]{:S(2)}) async-start(f32[32,1,3072]{2,1,0:T(1,128)} %reshape.321), calls=%async_computation | async-start | bytes 786432 | tf_op jit(solution)/shard_map/all_to_all | solution.py:15
  14.8 0.6 copy-done.4
  15.5 0.6 copy-done.3
  16.1 0.7 add_convert_fusion.3.pick_x_ref
  16.9 0.7 add_convert_fusion.pick_y_ref
  17.6 0.7 add_convert_fusion.1.pick_z_ref
  18.3 0.6 add_convert_fusion.2.onehot_ref
  18.9 9.2 %all-to-all-done = f32[32,1,3072]{2,1,0:T(1,128)S(1)} async-done(((f32[32,1,3072]{2,1,0:T(1,128)}), f32[32,1,3072]{2,1,0:T(1,128)S(1)}, u32[]{:S(2)}, u32[]{:S(2)}) %all-to-all-start) | async-done | bytes 393248 | tf_op jit(solution)/shard_map/all_to_all | solution.py:15
  28.2 0.5 broadcast.106
  28.7 1.5 %reduce = f32[32,3072]{1,0:T(8,128)S(1)} reduce(f32[32,1,3072]{2,1,0:T(1,128)S(1)} %all-to-all-done, f32[]{:T(128)} %broadcast.106), dimensions={1}, to_apply=%all_to_all.19.reduce_sub_computation | reduce | bytes 786436 | tf_op jit(solution)/shard_map/all_to_all | solution.py:15
  31.0 1.5 %fusion.3 = (f32[16,3,1,2048]{3,0,2,1:T(8,128)S(1)}, f32[16,3,1,2048]{3,0,2,1:T(8,128)S(1)}) fusion(f32[16,3,1,2048]{3,0,2,1:T(8,128)S(1)} %reshape.314), kind=kLoop, calls=%fused_computation.8 | loop fusion | flops 294912 | bytes 1179648 | tf_op jit(solution)/shard_map/cos | solution.py:166
  32.5 1.4 %copy.28.base_ref = f32[16,6,2048]{2,1,0:T(8,128)} copy(f32[16,6,2048]{2,0,1:T(8,128)S(1)} %bitcast.63) | data formatting | bytes 1572864 | tf_op jit(solution)/shard_map/reshape | solution.py:166
  34.0 30.6 %shard_map.59 = f32[16,2,2,16,128]{4,3,2,1,0:T(8,128)} custom-call(f32[16,6,2048]{2,1,0:T(8,128)} %copy.28.base_ref, f32[2,2048]{1,0:T(2,128)} %add_convert_fusion.2.onehot_ref, bf16[16,32]{1,0:T(8,128)(2,1)} %add_convert_fusion.3.pick_x_ref, bf16[128,96]{1,0:T(8,128)(2,1)} %add_convert_fusion.pick_y_ref, bf16[128,96]{1,0:T(8,128)(2,1)} %add_convert_fusion.1.pick_z_ref), custom_call_target="tpu_custom_call" | custom-call | tf_op jit(solution)/shard_map/pallas_call | solution.py:172
  64.6 1.1 %copy.37 = f32[16,2,2,4,4,128]{5,4,2,1,0,3:T(4,128)S(1)} copy(f32[16,2,2,4,4,128]{5,4,3,2,1,0:T(4,128)} %bitcast.64) | data formatting | bytes 1048576 | tf_op jit(solution)/shard_map/reshape | solution.py:33
  65.7 13.4 %all_to_all.28 = f32[4,16,2,2,4,128]{5,4,3,2,1,0:T(4,128)S(1)} all-to-all(f32[4,16,2,2,4,128]{5,4,3,2,1,0:T(4,128)S(1)} %bitcast.65), channel_id=1, replica_groups=mesh['atom'=4,'tm'=4,'wave'=32] {'atom'}, dimensions={0} | all-to-all | bytes 1048576 | tf_op jit(solution)/shard_map/all_to_all | solution.py:39
  79.3 0.7 copy.30
  80.0 6.2 %all-to-all-start.2 = ((f32[16,2,2,4,128]{4,0,2,1,3:T(8,128)}), f32[16,2,2,4,128]{4,0,2,1,3:T(8,128)S(1)}, u32[]{:S(2)}, u32[]{:S(2)}) async-start(f32[16,2,2,4,128]{4,0,2,1,3:T(8,128)} %copy.30), calls=%async_computation.2 | async-start | bytes 262144 | tf_op jit(solution)/shard_map/all_to_all | solution.py:193
  86.2 0.7 multiply_reduce_fusion
  86.9 7.7 %all-to-all-done.2 = f32[16,2,2,4,128]{4,0,2,1,3:T(8,128)S(1)} async-done(((f32[16,2,2,4,128]{4,0,2,1,3:T(8,128)}), f32[16,2,2,4,128]{4,0,2,1,3:T(8,128)S(1)}, u32[]{:S(2)}, u32[]{:S(2)}) %all-to-all-start.2) | async-done | bytes 131104 | tf_op jit(solution)/shard_map/all_to_all | solution.py:193
  95.4 0.3 fusion
  95.7 0.3 convolution_add_fusion
  96.1 1.2 %maximum_divide_fusion = f32[3,64,1,128]{3,1,2,0:T(8,128)} fusion(f32[1,64,1,128]{3,1,2,0:T(8,128)S(1)} %fusion.9, f32[1,64,1,128]{3,1,2,0:T(8,128)S(1)} %get-tuple-element.13, f32[1,64,1,128]{3,1,2,0:T(8,128)S(1)} %get-tuple-element.12, f32[]{:T(128)} %multiply_reduce_fusion), kind=kLoop, calls=%fused_computation.9 | loop fusion | flops 73728 | bytes 196612 | tf_op jit(solution)/shard_map/div | solution.py:80
  (29 shorter events, 2.1 us)
Async XLA Ops:
  0.6 0.7 copy-start
  2.7 12.1 %copy-start.2 = (s32[2048]{0:T(1024)S(1)}, s32[2048]{0:T(1024)}, u32[]{:S(2)}) copy-start(s32[2048]{0:T(1024)} %param.5) | copy-start | bytes 24580
  2.7 25.5 %all-to-all-start = ((f32[32,1,3072]{2,1,0:T(1,128)}), f32[32,1,3072]{2,1,0:T(1,128)S(1)}, u32[]{:S(2)}, u32[]{:S(2)}) async-start(f32[32,1,3072]{2,1,0:T(1,128)} %reshape.321), calls=%async_computation | async-start | bytes 786432 | tf_op jit(solution)/shard_map/all_to_all | solution.py:15
  14.8 0.7 copy-start.4
  15.4 0.7 copy-start.3
  79.3 0.7 copy-start.1
  80.0 14.6 %all-to-all-start.2 = ((f32[16,2,2,4,128]{4,0,2,1,3:T(8,128)}), f32[16,2,2,4,128]{4,0,2,1,3:T(8,128)S(1)}, u32[]{:S(2)}, u32[]{:S(2)}) async-start(f32[16,2,2,4,128]{4,0,2,1,3:T(8,128)} %copy.30), calls=%async_computation.2 | async-start | bytes 262144 | tf_op jit(solution)/shard_map/all_to_all | solution.py:193

commit v6 on v5

--- a/solution.py
+++ b/solution.py
@@ -165,7 +165,7 @@
     angle = TWO_PI * frac_turns(block_coords)
     base = jnp.stack([jnp.cos(angle), jnp.sin(angle)], axis=2).reshape(local_frames, 6, atom_count)
     rows_pad = 48
-    frames_per_step = math.gcd(local_frames, 4)
+    frames_per_step = math.gcd(local_frames, 8)
     pick_x = picks_of(kx_index, 1, 16)
     pick_y = picks_of(kyz_index[0], -16, rows_pad)
     pick_z = picks_of(kyz_index[1], -16, rows_pad)

time: 97.8 us -> 96.7 us (0.989)
  Pallas kernels: 30.6 us -> 29.5 us
    pallas_call x1, Pallas kernels: 30.6 us -> 29.5 us  [local(): pl.pallas_call(frame_kernel, grid=(local_frames // frames_per_step,), in_...]
where the time goes in v6:
time: 96.7 us; the launch traced here: 96.2 us
  Pallas kernels  29.5 us (31%)
  starting transfers between devices  18.3 us (19%)
  waiting for transfers between devices  16.9 us (17%)
  blocking collectives  13.4 us (14%)
  other arithmetic  8.05 us (8%)
  local copies, waits for them, and re-layouts  7.88 us (8%)
  matrix products  1.33 us (1%)
    pallas_call x1, Pallas kernels, local(): pl.pallas_call(frame_kernel, grid=(local_frames // frames_per_step,), in_...  29.5 us
    all_to_all x1, blocking collectives, sent_and_summed(): lax.all_to_all(pieces, axis, split_axis=0, concat_axis=0, tiled=True)  13.4 us
    all_to_all x1, starting transfers between devices, copy_for_each(): lax.all_to_all(jnp.broadcast_to(shard[None], (peers, *shard.shape)), axis...  12.1 us
    all_to_all x1, waiting for transfers between devices, copy_for_each(): lax.all_to_all(jnp.broadcast_to(shard[None], (peers, *shard.shape)), axis...  9.23 us
    all_to_all x1, waiting for transfers between devices, local(): lax.all_to_all(densities, 'tm', split_axis=3, concat_axis=0, tiled=True)  7.68 us
    all_to_all x1, starting transfers between devices, local(): lax.all_to_all(densities, 'tm', split_axis=3, concat_axis=0, tiled=True)  6.2 us
    unnamed x13, local copies, waits for them, and re-layouts  3.46 us
    concatenate x3, other arithmetic, picks_of(): return jnp.concatenate([picks, picks], axis=1)  2.08 us
  transfers between devices with their start and end apart: 2, of which 2 were waited for; matrix products, arithmetic and copies ran while one was open for 4% of the time, Pallas kernels for 0%

profile of v6, /device:TPU:8, one launch (start us, length us, event | category | flops | bytes accessed | tf_op | source)
XLA Modules:
  0.0 96.2 jit_solution(18036330824869354829)
XLA Ops:
  0.6 0.7 copy-done
  1.4 1.2 %reshape.321 = f32[32,1,3072]{2,1,0:T(1,128)} reshape(f32[32,3,16,64]{3,2,1,0:T(8,128)S(1)} %broadcast_bitcast_fusion) | data formatting | bytes 786432
  2.7 12.1 %all-to-all-start = ((f32[32,1,3072]{2,1,0:T(1,128)}), f32[32,1,3072]{2,1,0:T(1,128)S(1)}, u32[]{:S(2)}, u32[]{:S(2)}) async-start(f32[32,1,3072]{2,1,0:T(1,128)} %reshape.321), calls=%async_computation | async-start | bytes 786432 | tf_op jit(solution)/shard_map/all_to_all | solution.py:15
  14.8 0.6 copy-done.4
  15.5 0.6 copy-done.3
  16.1 0.7 add_convert_fusion.3.pick_x_ref
  16.9 0.7 add_convert_fusion.pick_y_ref
  17.6 0.7 add_convert_fusion.1.pick_z_ref
  18.3 0.6 add_convert_fusion.2.onehot_ref
  18.9 9.2 %all-to-all-done = f32[32,1,3072]{2,1,0:T(1,128)S(1)} async-done(((f32[32,1,3072]{2,1,0:T(1,128)}), f32[32,1,3072]{2,1,0:T(1,128)S(1)}, u32[]{:S(2)}, u32[]{:S(2)}) %all-to-all-start) | async-done | bytes 393248 | tf_op jit(solution)/shard_map/all_to_all | solution.py:15
  28.2 0.5 broadcast.106
  28.7 1.5 %reduce = f32[32,3072]{1,0:T(8,128)S(1)} reduce(f32[32,1,3072]{2,1,0:T(1,128)S(1)} %all-to-all-done, f32[]{:T(128)} %broadcast.106), dimensions={1}, to_apply=%all_to_all.19.reduce_sub_computation | reduce | bytes 786436 | tf_op jit(solution)/shard_map/all_to_all | solution.py:15
  31.0 1.5 %fusion.3 = (f32[16,3,1,2048]{3,0,2,1:T(8,128)S(1)}, f32[16,3,1,2048]{3,0,2,1:T(8,128)S(1)}) fusion(f32[16,3,1,2048]{3,0,2,1:T(8,128)S(1)} %reshape.314), kind=kLoop, calls=%fused_computation.8 | loop fusion | flops 294912 | bytes 1179648 | tf_op jit(solution)/shard_map/cos | solution.py:166
  32.5 1.4 %copy.28.base_ref = f32[16,6,2048]{2,1,0:T(8,128)} copy(f32[16,6,2048]{2,0,1:T(8,128)S(1)} %bitcast.63) | data formatting | bytes 1572864 | tf_op jit(solution)/shard_map/reshape | solution.py:166
  34.0 29.5 %shard_map.59 = f32[16,2,2,16,128]{4,3,2,1,0:T(8,128)} custom-call(f32[16,6,2048]{2,1,0:T(8,128)} %copy.28.base_ref, f32[2,2048]{1,0:T(2,128)} %add_convert_fusion.2.onehot_ref, bf16[16,32]{1,0:T(8,128)(2,1)} %add_convert_fusion.3.pick_x_ref, bf16[128,96]{1,0:T(8,128)(2,1)} %add_convert_fusion.pick_y_ref, bf16[128,96]{1,0:T(8,128)(2,1)} %add_convert_fusion.1.pick_z_ref), custom_call_target="tpu_custom_call" | custom-call | tf_op jit(solution)/shard_map/pallas_call | solution.py:172
  63.4 1.1 %copy.37 = f32[16,2,2,4,4,128]{5,4,2,1,0,3:T(4,128)S(1)} copy(f32[16,2,2,4,4,128]{5,4,3,2,1,0:T(4,128)} %bitcast.64) | data formatting | bytes 1048576 | tf_op jit(solution)/shard_map/reshape | solution.py:33
  64.6 13.4 %all_to_all.28 = f32[4,16,2,2,4,128]{5,4,3,2,1,0:T(4,128)S(1)} all-to-all(f32[4,16,2,2,4,128]{5,4,3,2,1,0:T(4,128)S(1)} %bitcast.65), channel_id=1, replica_groups=mesh['atom'=4,'tm'=4,'wave'=32] {'atom'}, dimensions={0} | all-to-all | bytes 1048576 | tf_op jit(solution)/shard_map/all_to_all | solution.py:39
  78.2 0.7 copy.30
  78.9 6.2 %all-to-all-start.2 = ((f32[16,2,2,4,128]{4,0,2,1,3:T(8,128)}), f32[16,2,2,4,128]{4,0,2,1,3:T(8,128)S(1)}, u32[]{:S(2)}, u32[]{:S(2)}) async-start(f32[16,2,2,4,128]{4,0,2,1,3:T(8,128)} %copy.30), calls=%async_computation.2 | async-start | bytes 262144 | tf_op jit(solution)/shard_map/all_to_all | solution.py:193
  85.1 0.7 multiply_reduce_fusion
  85.8 7.7 %all-to-all-done.2 = f32[16,2,2,4,128]{4,0,2,1,3:T(8,128)S(1)} async-done(((f32[16,2,2,4,128]{4,0,2,1,3:T(8,128)}), f32[16,2,2,4,128]{4,0,2,1,3:T(8,128)S(1)}, u32[]{:S(2)}, u32[]{:S(2)}) %all-to-all-start.2) | async-done | bytes 131104 | tf_op jit(solution)/shard_map/all_to_all | solution.py:193
  94.2 0.3 fusion
  94.6 0.3 convolution_add_fusion
  94.9 1.2 %maximum_divide_fusion = f32[3,64,1,128]{3,1,2,0:T(8,128)} fusion(f32[1,64,1,128]{3,1,2,0:T(8,128)S(1)} %fusion.9, f32[1,64,1,128]{3,1,2,0:T(8,128)S(1)} %get-tuple-element.13, f32[1,64,1,128]{3,1,2,0:T(8,128)S(1)} %get-tuple-element.12, f32[]{:T(128)} %multiply_reduce_fusion), kind=kLoop, calls=%fused_computation.9 | loop fusion | flops 73728 | bytes 196612 | tf_op jit(solution)/shard_map/div | solution.py:80
  (29 shorter events, 2.1 us)
Async XLA Ops:
  0.6 0.7 copy-start
  2.7 12.1 %copy-start.2 = (s32[2048]{0:T(1024)S(1)}, s32[2048]{0:T(1024)}, u32[]{:S(2)}) copy-start(s32[2048]{0:T(1024)} %param.5) | copy-start | bytes 24580
  2.7 25.5 %all-to-all-start = ((f32[32,1,3072]{2,1,0:T(1,128)}), f32[32,1,3072]{2,1,0:T(1,128)S(1)}, u32[]{:S(2)}, u32[]{:S(2)}) async-start(f32[32,1,3072]{2,1,0:T(1,128)} %reshape.321), calls=%async_computation | async-start | bytes 786432 | tf_op jit(solution)/shard_map/all_to_all | solution.py:15
  14.8 0.7 copy-start.4
  15.4 0.7 copy-start.3
  78.2 0.7 copy-start.1
  78.9 14.6 %all-to-all-start.2 = ((f32[16,2,2,4,128]{4,0,2,1,3:T(8,128)}), f32[16,2,2,4,128]{4,0,2,1,3:T(8,128)S(1)}, u32[]{:S(2)}, u32[]{:S(2)}) async-start(f32[16,2,2,4,128]{4,0,2,1,3:T(8,128)} %copy.30), calls=%async_computation.2 | async-start | bytes 262144 | tf_op jit(solution)/shard_map/all_to_all | solution.py:193

commit v7 on v6

--- a/solution.py
+++ b/solution.py
@@ -160,10 +160,10 @@
     kyz_local = kyz_index.shape[1]
     total_atoms = positions.shape[2] * lax.axis_size("atom") * lax.axis_size("wave")
     onehot_all = jnp.stack([species == 0, species == 1]).astype(jnp.float32)
-    block_coords = gathered_copies(positions, "wave", 2)
-    atom_count = block_coords.shape[2]
-    angle = TWO_PI * frac_turns(block_coords)
-    base = jnp.stack([jnp.cos(angle), jnp.sin(angle)], axis=2).reshape(local_frames, 6, atom_count)
+    angle = TWO_PI * frac_turns(positions)
+    local_base = jnp.stack([jnp.cos(angle), jnp.sin(angle)], axis=2).reshape(local_frames, 6, positions.shape[2])
+    base = gathered_copies(local_base, "wave", 2)
+    atom_count = base.shape[2]
     rows_pad = 48
     frames_per_step = math.gcd(local_frames, 8)
     pick_x = picks_of(kx_index, 1, 16)

time: 96.7 us -> 106 us (1.096)
  the two profiles are of different devices: /device:TPU:8 before, /device:TPU:64 now
where the time goes in v7:
time: 106 us
  Pallas kernels  29.5 us (28%)
  waiting for transfers between devices  27.6 us (26%)
  starting transfers between devices  17.3 us (16%)
  blocking collectives  13.1 us (12%)
  other arithmetic  8.47 us (8%)
  local copies, waits for them, and re-layouts  7.57 us (7%)
  matrix products  1.33 us (1%)
    pallas_call x1, Pallas kernels, local(): pl.pallas_call(frame_kernel, grid=(local_frames // frames_per_step,), in_...  29.5 us
    all_to_all x1, waiting for transfers between devices, copy_for_each(): lax.all_to_all(jnp.broadcast_to(shard[None], (peers, *shard.shape)), axis...  19.2 us
    all_to_all x1, blocking collectives, sent_and_summed(): lax.all_to_all(pieces, axis, split_axis=0, concat_axis=0, tiled=True)  13.1 us
    all_to_all x1, starting transfers between devices, copy_for_each(): lax.all_to_all(jnp.broadcast_to(shard[None], (peers, *shard.shape)), axis...  11.1 us
    all_to_all x1, waiting for transfers between devices, local(): lax.all_to_all(densities, 'tm', split_axis=3, concat_axis=0, tiled=True)  8.36 us
    all_to_all x1, starting transfers between devices, local(): lax.all_to_all(densities, 'tm', split_axis=3, concat_axis=0, tiled=True)  6.2 us
    unnamed x11, local copies, waits for them, and re-layouts  2.68 us
    all_to_all x1, other arithmetic, copy_for_each(): lax.all_to_all(jnp.broadcast_to(shard[None], (peers, *shard.shape)), axis...  2.48 us
  transfers between devices with their start and end apart: 2, of which 2 were waited for; matrix products, arithmetic and copies ran while one was open for 3% of the time, Pallas kernels for 0%

profile of v7, /device:TPU:64, one launch (start us, length us, event | category | flops | bytes accessed | tf_op | source)
XLA Modules:
  0.0 105.7 jit_solution(9784429810678172803)
XLA Ops:
  0.6 0.8 cosine_bitcast_fusion
  1.7 1.9 %reshape.283 = f32[32,1,6144]{2,1,0:T(1,128)} reshape(f32[32,6,16,64]{3,2,1,0:T(8,128)S(1)} %broadcast_bitcast_fusion) | data formatting | bytes 1572864
  3.6 11.1 %all-to-all-start = ((f32[32,1,6144]{2,1,0:T(1,128)}), f32[32,1,6144]{2,1,0:T(1,128)S(1)}, u32[]{:S(2)}, u32[]{:S(2)}) async-start(f32[32,1,6144]{2,1,0:T(1,128)} %reshape.283), calls=%async_computation | async-start | bytes 1572864 | tf_op jit(solution)/shard_map/all_to_all | solution.py:15
  14.9 0.7 add_convert_fusion.3.pick_x_ref
  15.7 0.7 add_convert_fusion.pick_y_ref
  16.4 0.7 add_convert_fusion.1.pick_z_ref
  17.1 0.6 add_convert_fusion.2.onehot_ref
  17.7 19.2 %all-to-all-done = f32[32,1,6144]{2,1,0:T(1,128)S(1)} async-done(((f32[32,1,6144]{2,1,0:T(1,128)}), f32[32,1,6144]{2,1,0:T(1,128)S(1)}, u32[]{:S(2)}, u32[]{:S(2)}) %all-to-all-start) | async-done | bytes 786464 | tf_op jit(solution)/shard_map/all_to_all | solution.py:15
  36.9 0.5 broadcast.94
  37.4 2.5 %reduce = f32[32,6144]{1,0:T(8,128)S(1)} reduce(f32[32,1,6144]{2,1,0:T(1,128)S(1)} %all-to-all-done, f32[]{:T(128)} %broadcast.94), dimensions={1}, to_apply=%all_to_all.19.reduce_sub_computation | reduce | bytes 1572868 | tf_op jit(solution)/shard_map/all_to_all | solution.py:15
  39.9 0.6 reshape.284
  40.7 0.9 copy.38
  41.6 1.5 %reshape.282.base_ref = f32[16,6,2048]{2,1,0:T(8,128)} reshape(f32[16,6,32,64]{3,2,1,0:T(8,128)S(1)} %copy.38) | data formatting | bytes 1572864 | tf_op jit(solution)/shard_map/reshape | solution.py:23
  43.1 29.5 %shard_map.59 = f32[16,2,2,16,128]{4,3,2,1,0:T(8,128)} custom-call(f32[16,6,2048]{2,1,0:T(8,128)} %reshape.282.base_ref, f32[2,2048]{1,0:T(2,128)} %add_convert_fusion.2.onehot_ref, bf16[16,32]{1,0:T(8,128)(2,1)} %add_convert_fusion.3.pick_x_ref, bf16[128,96]{1,0:T(8,128)(2,1)} %add_convert_fusion.pick_y_ref, bf16[128,96]{1,0:T(8,128)(2,1)} %add_convert_fusion.1.pick_z_ref), custom_call_target="tpu_custom_call" | custom-call | tf_op jit(solution)/shard_map/pallas_call | solution.py:172
  72.6 1.1 %copy.41 = f32[16,2,2,4,4,128]{5,4,2,1,0,3:T(4,128)S(1)} copy(f32[16,2,2,4,4,128]{5,4,3,2,1,0:T(4,128)} %bitcast.67) | data formatting | bytes 1048576 | tf_op jit(solution)/shard_map/reshape | solution.py:33
  73.7 13.1 %all_to_all.28 = f32[4,16,2,2,4,128]{5,4,3,2,1,0:T(4,128)S(1)} all-to-all(f32[4,16,2,2,4,128]{5,4,3,2,1,0:T(4,128)S(1)} %bitcast.68), channel_id=1, replica_groups=mesh['atom'=4,'tm'=4,'wave'=32] {'atom'}, dimensions={0} | all-to-all | bytes 1048576 | tf_op jit(solution)/shard_map/all_to_all | solution.py:39
  87.0 0.7 copy.32
  87.7 6.2 %all-to-all-start.2 = ((f32[16,2,2,4,128]{4,0,2,1,3:T(8,128)}), f32[16,2,2,4,128]{4,0,2,1,3:T(8,128)S(1)}, u32[]{:S(2)}, u32[]{:S(2)}) async-start(f32[16,2,2,4,128]{4,0,2,1,3:T(8,128)} %copy.32), calls=%async_computation.2 | async-start | bytes 262144 | tf_op jit(solution)/shard_map/all_to_all | solution.py:193
  93.9 0.7 multiply_reduce_fusion
  94.6 8.4 %all-to-all-done.2 = f32[16,2,2,4,128]{4,0,2,1,3:T(8,128)S(1)} async-done(((f32[16,2,2,4,128]{4,0,2,1,3:T(8,128)}), f32[16,2,2,4,128]{4,0,2,1,3:T(8,128)S(1)}, u32[]{:S(2)}, u32[]{:S(2)}) %all-to-all-start.2) | async-done | bytes 131104 | tf_op jit(solution)/shard_map/all_to_all | solution.py:193
  103.4 0.3 fusion.1
  103.7 0.3 fusion
  104.1 0.3 convolution_add_fusion
  104.4 1.3 %maximum_divide_fusion = f32[3,64,1,128]{3,1,2,0:T(8,128)} fusion(f32[1,64,1,128]{3,1,2,0:T(8,128)S(1)} %fusion.6, f32[1,64,1,128]{3,1,2,0:T(8,128)S(1)} %get-tuple-element.11, f32[1,64,1,128]{3,1,2,0:T(8,128)S(1)} %get-tuple-element.10, f32[]{:T(128)} %multiply_reduce_fusion), kind=kLoop, calls=%fused_computation.4 | loop fusion | flops 73728 | bytes 196612 | tf_op jit(solution)/shard_map/div | solution.py:80
  (26 shorter events, 1.2 us)
Async XLA Ops:
  1.7 13.0 %copy-start.1 = (s32[2048]{0:T(1024)S(1)}, s32[2048]{0:T(1024)}, u32[]{:S(2)}) copy-start(s32[2048]{0:T(1024)} %param.5) | copy-start | bytes 24580
  1.7 13.1 %copy-start.3 = (s32[16]{0:T(128)S(1)}, s32[16]{0:T(128)}, u32[]{:S(2)}) copy-start(s32[16]{0:T(128)} %param.6) | copy-start | bytes 196
  1.7 13.9 %copy-start.2 = (s32[2,128]{1,0:T(2,128)S(1)}, s32[2,128]{1,0:T(2,128)}, u32[]{:S(2)}) copy-start(s32[2,128]{1,0:T(2,128)} %param.7) | copy-start | bytes 3076
  3.6 33.4 %all-to-all-start = ((f32[32,1,6144]{2,1,0:T(1,128)}), f32[32,1,6144]{2,1,0:T(1,128)S(1)}, u32[]{:S(2)}, u32[]{:S(2)}) async-start(f32[32,1,6144]{2,1,0:T(1,128)} %reshape.283), calls=%async_computation | async-start | bytes 1572864 | tf_op jit(solution)/shard_map/all_to_all | solution.py:15
  87.0 18.8 %copy-start = (f32[16,2,2,4,128]{4,3,2,1,0:T(4,128)}, f32[16,2,2,4,128]{4,3,2,1,0:T(4,128)S(1)}, u32[]{:S(2)}) copy-start(f32[16,2,2,4,128]{4,3,2,1,0:T(4,128)S(1)} %broadcast_multiply_fusion.1) | copy-start | bytes 393220
  87.7 15.3 %all-to-all-start.2 = ((f32[16,2,2,4,128]{4,0,2,1,3:T(8,128)}), f32[16,2,2,4,128]{4,0,2,1,3:T(8,128)S(1)}, u32[]{:S(2)}, u32[]{:S(2)}) async-start(f32[16,2,2,4,128]{4,0,2,1,3:T(8,128)} %copy.32), calls=%async_computation.2 | async-start | bytes 262144 | tf_op jit(solution)/shard_map/all_to_all | solution.py:193

commit v8 on v6

--- a/solution.py
+++ b/solution.py
@@ -160,7 +160,11 @@
     kyz_local = kyz_index.shape[1]
     total_atoms = positions.shape[2] * lax.axis_size("atom") * lax.axis_size("wave")
     onehot_all = jnp.stack([species == 0, species == 1]).astype(jnp.float32)
-    block_coords = gathered_copies(positions, "wave", 2)
+    flat = positions.size
+    lane_rows = flat // 128 if flat % 128 == 0 else 1
+    packed = copy_for_each(positions.reshape(lane_rows, flat // lane_rows), "wave")
+    peers = lax.axis_size("wave")
+    block_coords = joined_along(packed.reshape(peers, *positions.shape), 2)
     atom_count = block_coords.shape[2]
     angle = TWO_PI * frac_turns(block_coords)
     base = jnp.stack([jnp.cos(angle), jnp.sin(angle)], axis=2).reshape(local_frames, 6, atom_count)

time: 96.7 us -> 94.7 us (0.979)
  other arithmetic: 8.05 us -> 6.66 us
    all_to_all x1 -> x0, other arithmetic: 1.5 us -> none  [copy_for_each(): lax.all_to_all(jnp.broadcast_to(shard[None], (peers, *shard.shape)), axis...]
    unnamed x13 -> x9, local copies, waits for them, and re-layouts: 3.46 us -> 2 us
where the time goes in v8:
time: 94.7 us; the launch traced here: 94.2 us
  Pallas kernels  29.5 us (31%)
  starting transfers between devices  18.3 us (19%)
  waiting for transfers between devices  16.9 us (18%)
  blocking collectives  13.4 us (14%)
  local copies, waits for them, and re-layouts  7.38 us (8%)
  other arithmetic  6.66 us (7%)
  matrix products  1.33 us (1%)
    pallas_call x1, Pallas kernels, local(): pl.pallas_call(frame_kernel, grid=(local_frames // frames_per_step,), in_...  29.5 us
    all_to_all x1, blocking collectives, sent_and_summed(): lax.all_to_all(pieces, axis, split_axis=0, concat_axis=0, tiled=True)  13.4 us
    all_to_all x1, starting transfers between devices, copy_for_each(): lax.all_to_all(jnp.broadcast_to(shard[None], (peers, *shard.shape)), axis...  12.1 us
    all_to_all x1, waiting for transfers between devices, copy_for_each(): lax.all_to_all(jnp.broadcast_to(shard[None], (peers, *shard.shape)), axis...  9.25 us
    all_to_all x1, waiting for transfers between devices, local(): lax.all_to_all(densities, 'tm', split_axis=3, concat_axis=0, tiled=True)  7.62 us
    all_to_all x1, starting transfers between devices, local(): lax.all_to_all(densities, 'tm', split_axis=3, concat_axis=0, tiled=True)  6.19 us
    concatenate x3, other arithmetic, picks_of(): return jnp.concatenate([picks, picks], axis=1)  2.07 us
    unnamed x9, local copies, waits for them, and re-layouts  2 us
  transfers between devices with their start and end apart: 2, of which 2 were waited for; matrix products, arithmetic and copies ran while one was open for 4% of the time, Pallas kernels for 0%

profile of v8, /device:TPU:8, one launch (start us, length us, event | category | flops | bytes accessed | tf_op | source)
XLA Modules:
  0.0 94.2 jit_solution(9547429862629572187)
XLA Ops:
  0.6 0.8 copy.38
  1.5 0.8 broadcast_in_dim.5
  2.2 12.1 %all-to-all-start = ((f32[32,24,128]{2,1,0:T(8,128)}), f32[32,24,128]{2,1,0:T(8,128)S(1)}, u32[]{:S(2)}, u32[]{:S(2)}) async-start(f32[32,24,128]{2,1,0:T(8,128)} %broadcast_in_dim.5), calls=%async_computation | async-start | bytes 786432 | tf_op jit(solution)/shard_map/all_to_all | solution.py:15
  14.4 0.6 copy-done.3
  15.1 0.6 copy-done.2
  15.7 0.7 add_convert_fusion.3.pick_x_ref
  16.5 0.7 add_convert_fusion.pick_y_ref
  17.2 0.7 add_convert_fusion.1.pick_z_ref
  17.9 0.6 add_convert_fusion.2.onehot_ref
  18.5 9.2 %all-to-all-done = f32[32,24,128]{2,1,0:T(8,128)S(1)} async-done(((f32[32,24,128]{2,1,0:T(8,128)}), f32[32,24,128]{2,1,0:T(8,128)S(1)}, u32[]{:S(2)}, u32[]{:S(2)}) %all-to-all-start) | async-done | bytes 393248 | tf_op jit(solution)/shard_map/all_to_all | solution.py:15
  27.8 0.4 reshape.317
  28.2 0.5 copy.39
  28.9 1.5 %fusion.3 = (f32[16,3,1,2048]{3,0,1,2:T(8,128)S(1)}, f32[16,3,1,2048]{3,0,1,2:T(8,128)S(1)}) fusion(f32[16,3,1,2048]{3,0,1,2:T(8,128)S(1)} %reshape.318), kind=kLoop, calls=%fused_computation.8 | loop fusion | flops 294912 | bytes 1179648 | tf_op jit(solution)/shard_map/cos | solution.py:170
  30.5 1.4 %copy.41.base_ref = f32[16,6,2048]{2,1,0:T(8,128)} copy(f32[16,6,2048]{2,0,1:T(8,128)S(1)} %bitcast.59) | data formatting | bytes 1572864 | tf_op jit(solution)/shard_map/reshape | solution.py:170
  32.0 29.5 %shard_map.59 = f32[16,2,2,16,128]{4,3,2,1,0:T(8,128)} custom-call(f32[16,6,2048]{2,1,0:T(8,128)} %copy.41.base_ref, f32[2,2048]{1,0:T(2,128)} %add_convert_fusion.2.onehot_ref, bf16[16,32]{1,0:T(8,128)(2,1)} %add_convert_fusion.3.pick_x_ref, bf16[128,96]{1,0:T(8,128)(2,1)} %add_convert_fusion.pick_y_ref, bf16[128,96]{1,0:T(8,128)(2,1)} %add_convert_fusion.1.pick_z_ref), custom_call_target="tpu_custom_call" | custom-call | tf_op jit(solution)/shard_map/pallas_call | solution.py:176
  61.4 1.1 %copy.50 = f32[16,2,2,4,4,128]{5,4,2,1,0,3:T(4,128)S(1)} copy(f32[16,2,2,4,4,128]{5,4,3,2,1,0:T(4,128)} %bitcast.60) | data formatting | bytes 1048576 | tf_op jit(solution)/shard_map/reshape | solution.py:33
  62.6 13.4 %all_to_all.28 = f32[4,16,2,2,4,128]{5,4,3,2,1,0:T(4,128)S(1)} all-to-all(f32[4,16,2,2,4,128]{5,4,3,2,1,0:T(4,128)S(1)} %bitcast.61), channel_id=1, replica_groups=mesh['atom'=4,'tm'=4,'wave'=32] {'atom'}, dimensions={0} | all-to-all | bytes 1048576 | tf_op jit(solution)/shard_map/all_to_all | solution.py:39
  76.1 0.7 copy.43
  76.9 6.2 %all-to-all-start.2 = ((f32[16,2,2,4,128]{4,0,2,1,3:T(8,128)}), f32[16,2,2,4,128]{4,0,2,1,3:T(8,128)S(1)}, u32[]{:S(2)}, u32[]{:S(2)}) async-start(f32[16,2,2,4,128]{4,0,2,1,3:T(8,128)} %copy.43), calls=%async_computation.2 | async-start | bytes 262144 | tf_op jit(solution)/shard_map/all_to_all | solution.py:197
  83.0 0.7 multiply_reduce_fusion
  83.8 7.6 %all-to-all-done.2 = f32[16,2,2,4,128]{4,0,2,1,3:T(8,128)S(1)} async-done(((f32[16,2,2,4,128]{4,0,2,1,3:T(8,128)}), f32[16,2,2,4,128]{4,0,2,1,3:T(8,128)S(1)}, u32[]{:S(2)}, u32[]{:S(2)}) %all-to-all-start.2) | async-done | bytes 131104 | tf_op jit(solution)/shard_map/all_to_all | solution.py:197
  92.2 0.3 fusion
  92.5 0.3 convolution_add_fusion
  92.9 1.3 %maximum_divide_fusion = f32[3,64,1,128]{3,1,2,0:T(8,128)} fusion(f32[1,64,1,128]{3,1,2,0:T(8,128)S(1)} %fusion.9, f32[1,64,1,128]{3,1,2,0:T(8,128)S(1)} %get-tuple-element.15, f32[1,64,1,128]{3,1,2,0:T(8,128)S(1)} %get-tuple-element.14, f32[]{:T(128)} %multiply_reduce_fusion), kind=kLoop, calls=%fused_computation.9 | loop fusion | flops 73728 | bytes 196612 | tf_op jit(solution)/shard_map/div | solution.py:80
  (26 shorter events, 1.7 us)
Async XLA Ops:
  2.2 12.1 %copy-start.1 = (s32[2048]{0:T(1024)S(1)}, s32[2048]{0:T(1024)}, u32[]{:S(2)}) copy-start(s32[2048]{0:T(1024)} %param.5) | copy-start | bytes 24580
  2.2 25.5 %all-to-all-start = ((f32[32,24,128]{2,1,0:T(8,128)}), f32[32,24,128]{2,1,0:T(8,128)S(1)}, u32[]{:S(2)}, u32[]{:S(2)}) async-start(f32[32,24,128]{2,1,0:T(8,128)} %broadcast_in_dim.5), calls=%async_computation | async-start | bytes 786432 | tf_op jit(solution)/shard_map/all_to_all | solution.py:15
  14.4 0.7 copy-start.3
  15.0 0.7 copy-start.2
  76.1 0.7 copy-start
  76.9 14.6 %all-to-all-start.2 = ((f32[16,2,2,4,128]{4,0,2,1,3:T(8,128)}), f32[16,2,2,4,128]{4,0,2,1,3:T(8,128)S(1)}, u32[]{:S(2)}, u32[]{:S(2)}) async-start(f32[16,2,2,4,128]{4,0,2,1,3:T(8,128)} %copy.43), calls=%async_computation.2 | async-start | bytes 262144 | tf_op jit(solution)/shard_map/all_to_all | solution.py:197

commit v9 on v8

--- a/solution.py
+++ b/solution.py
@@ -144,8 +144,12 @@
     for s in range(2):
         cos_rows = slice((2 * s) * kx, (2 * s + 1) * kx)
         sin_rows = slice((2 * s + 1) * kx, (2 * s + 2) * kx)
-        out_ref[f, s, 0] = with_cos[cos_rows] - with_sin[sin_rows]
-        out_ref[f, s, 1] = -(with_sin[cos_rows] + with_cos[sin_rows])
+        real_part = with_cos[cos_rows] - with_sin[sin_rows]
+        imag_part = -(with_sin[cos_rows] + with_cos[sin_rows])
+        share = kx // out_ref.shape[0]
+        for peer in range(out_ref.shape[0]):
+            out_ref[peer, f, s, 0] = real_part[peer * share : (peer + 1) * share]
+            out_ref[peer, f, s, 1] = imag_part[peer * share : (peer + 1) * share]
 
 
 def picks_of(index, lowest, count):
@@ -169,6 +173,7 @@
     angle = TWO_PI * frac_turns(block_coords)
     base = jnp.stack([jnp.cos(angle), jnp.sin(angle)], axis=2).reshape(local_frames, 6, atom_count)
     rows_pad = 48
+    atom_peers = lax.axis_size("atom")
     frames_per_step = math.gcd(local_frames, 8)
     pick_x = picks_of(kx_index, 1, 16)
     pick_y = picks_of(kyz_index[0], -16, rows_pad)
@@ -183,8 +188,8 @@
             pl.BlockSpec((kyz_local, 2 * rows_pad), lambda t: (0, 0)),
             pl.BlockSpec((kyz_local, 2 * rows_pad), lambda t: (0, 0)),
         ],
-        out_specs=pl.BlockSpec((frames_per_step, 2, 2, kx_count, kyz_local), lambda t: (t, 0, 0, 0, 0)),
-        out_shape=jax.ShapeDtypeStruct((local_frames, 2, 2, kx_count, kyz_local), jnp.float32),
+        out_specs=pl.BlockSpec((atom_peers, frames_per_step, 2, 2, kx_count // atom_peers, kyz_local), lambda t: (0, t, 0, 0, 0, 0)),
+        out_shape=jax.ShapeDtypeStruct((atom_peers, local_frames, 2, 2, kx_count // atom_peers, kyz_local), jnp.float32),
         scratch_shapes=[
             pltpu.VMEM((frames_per_step, 4, rows_pad, atom_count), jnp.float32),
             pltpu.VMEM((frames_per_step, 2, 16, atom_count), jnp.float32),
@@ -192,7 +197,7 @@
             pltpu.VMEM((frames_per_step, 2, 32, atom_count), jnp.bfloat16),
         ],
     )(base, onehot_all, pick_x, pick_y, pick_z)
-    owned = sent_and_summed(partial_value, "atom", 3)
+    owned = lax.all_to_all(partial_value, "atom", split_axis=0, concat_axis=0, tiled=True).sum(axis=0)
     densities = owned / jnp.sqrt(jnp.float32(total_atoms))
     spectra = transform(lax.all_to_all(densities, "tm", split_axis=3, concat_axis=0, tiled=True))
     return (spectra, densities)

time: 94.7 us -> 93.8 us (level)
  local copies, waits for them, and re-layouts: 7.38 us -> 6.24 us
    reshape x1 -> x0, local copies, waits for them, and re-layouts: 1.14 us -> none  [cut_along(): shard.reshape(*dims[:dim], peers, dims[dim] // peers, *dims[dim + 1:])]
where the time goes in v9:
time: 93.8 us; the launch traced here: 93.3 us
  Pallas kernels  29.5 us (31%)
  starting transfers between devices  18.3 us (20%)
  waiting for transfers between devices  16.9 us (18%)
  blocking collectives  13.6 us (14%)
  other arithmetic  6.66 us (7%)
  local copies, waits for them, and re-layouts  6.24 us (7%)
  matrix products  1.33 us (1%)
    pallas_call x1, Pallas kernels, local(): pl.pallas_call(frame_kernel, grid=(local_frames // frames_per_step,), in_...  29.5 us
    all_to_all x1, blocking collectives, local(): lax.all_to_all(partial_value, 'atom', split_axis=0, concat_axis=0, tiled=...  13.6 us
    all_to_all x1, starting transfers between devices, copy_for_each(): lax.all_to_all(jnp.broadcast_to(shard[None], (peers, *shard.shape)), axis...  12.1 us
    all_to_all x1, waiting for transfers between devices, copy_for_each(): lax.all_to_all(jnp.broadcast_to(shard[None], (peers, *shard.shape)), axis...  9.25 us
    all_to_all x1, waiting for transfers between devices, local(): lax.all_to_all(densities, 'tm', split_axis=3, concat_axis=0, tiled=True)  7.62 us
    all_to_all x1, starting transfers between devices, local(): lax.all_to_all(densities, 'tm', split_axis=3, concat_axis=0, tiled=True)  6.19 us
    concatenate x3, other arithmetic, picks_of(): return jnp.concatenate([picks, picks], axis=1)  2.07 us
    unnamed x9, local copies, waits for them, and re-layouts  2 us
  transfers between devices with their start and end apart: 2, of which 2 were waited for; matrix products, arithmetic and copies ran while one was open for 4% of the time, Pallas kernels for 0%

profile of v9, /device:TPU:8, one launch (start us, length us, event | category | flops | bytes accessed | tf_op | source)
XLA Modules:
  0.0 93.3 jit_solution(3852884603406141449)
XLA Ops:
  0.6 0.8 copy.37
  1.5 0.8 broadcast_in_dim.5
  2.2 12.1 %all-to-all-start = ((f32[32,24,128]{2,1,0:T(8,128)}), f32[32,24,128]{2,1,0:T(8,128)S(1)}, u32[]{:S(2)}, u32[]{:S(2)}) async-start(f32[32,24,128]{2,1,0:T(8,128)} %broadcast_in_dim.5), calls=%async_computation | async-start | bytes 786432 | tf_op jit(solution)/shard_map/all_to_all | solution.py:15
  14.4 0.6 copy-done.3
  15.1 0.6 copy-done.2
  15.7 0.7 add_convert_fusion.3.pick_x_ref
  16.5 0.7 add_convert_fusion.pick_y_ref
  17.2 0.7 add_convert_fusion.1.pick_z_ref
  17.9 0.6 add_convert_fusion.2.onehot_ref
  18.5 9.2 %all-to-all-done = f32[32,24,128]{2,1,0:T(8,128)S(1)} async-done(((f32[32,24,128]{2,1,0:T(8,128)}), f32[32,24,128]{2,1,0:T(8,128)S(1)}, u32[]{:S(2)}, u32[]{:S(2)}) %all-to-all-start) | async-done | bytes 393248 | tf_op jit(solution)/shard_map/all_to_all | solution.py:15
  27.8 0.4 reshape.314
  28.2 0.5 copy.38
  28.9 1.5 %fusion.3 = (f32[16,3,1,2048]{3,0,1,2:T(8,128)S(1)}, f32[16,3,1,2048]{3,0,1,2:T(8,128)S(1)}) fusion(f32[16,3,1,2048]{3,0,1,2:T(8,128)S(1)} %reshape.315), kind=kLoop, calls=%fused_computation.7 | loop fusion | flops 294912 | bytes 1179648 | tf_op jit(solution)/shard_map/cos | solution.py:174
  30.5 1.4 %copy.40.base_ref = f32[16,6,2048]{2,1,0:T(8,128)} copy(f32[16,6,2048]{2,0,1:T(8,128)S(1)} %bitcast.55) | data formatting | bytes 1572864 | tf_op jit(solution)/shard_map/reshape | solution.py:174
  32.0 29.5 %shard_map.59 = f32[4,16,2,2,4,128]{5,4,3,2,1,0:T(4,128)} custom-call(f32[16,6,2048]{2,1,0:T(8,128)} %copy.40.base_ref, f32[2,2048]{1,0:T(2,128)} %add_convert_fusion.2.onehot_ref, bf16[16,32]{1,0:T(8,128)(2,1)} %add_convert_fusion.3.pick_x_ref, bf16[128,96]{1,0:T(8,128)(2,1)} %add_convert_fusion.pick_y_ref, bf16[128,96]{1,0:T(8,128)(2,1)} %add_convert_fusion.1.pick_z_ref), custom_call_target="tpu_custom_call" | custom-call | tf_op jit(solution)/shard_map/pallas_call | solution.py:181
  61.5 13.6 %all_to_all.28 = f32[4,16,2,2,4,128]{5,4,3,2,1,0:T(4,128)S(1)} all-to-all(f32[4,16,2,2,4,128]{5,4,3,2,1,0:T(4,128)} %shard_map.59), channel_id=1, replica_groups=mesh['atom'=4,'tm'=4,'wave'=32] {'atom'}, dimensions={0} | all-to-all | bytes 1048576 | tf_op jit(solution)/shard_map/all_to_all | solution.py:200
  75.3 0.7 copy.41
  76.0 6.2 %all-to-all-start.2 = ((f32[16,2,2,4,128]{4,0,2,1,3:T(8,128)}), f32[16,2,2,4,128]{4,0,2,1,3:T(8,128)S(1)}, u32[]{:S(2)}, u32[]{:S(2)}) async-start(f32[16,2,2,4,128]{4,0,2,1,3:T(8,128)} %copy.41), calls=%async_computation.2 | async-start | bytes 262144 | tf_op jit(solution)/shard_map/all_to_all | solution.py:202
  82.2 0.7 multiply_reduce_fusion
  82.9 7.6 %all-to-all-done.2 = f32[16,2,2,4,128]{4,0,2,1,3:T(8,128)S(1)} async-done(((f32[16,2,2,4,128]{4,0,2,1,3:T(8,128)}), f32[16,2,2,4,128]{4,0,2,1,3:T(8,128)S(1)}, u32[]{:S(2)}, u32[]{:S(2)}) %all-to-all-start.2) | async-done | bytes 131104 | tf_op jit(solution)/shard_map/all_to_all | solution.py:202
  91.0 0.3 fusion.4
  91.3 0.3 fusion
  91.7 0.3 convolution_add_fusion
  92.1 1.3 %maximum_divide_fusion = f32[3,64,1,128]{3,1,2,0:T(8,128)} fusion(f32[1,64,1,128]{3,1,2,0:T(8,128)S(1)} %fusion.9, f32[1,64,1,128]{3,1,2,0:T(8,128)S(1)} %get-tuple-element.15, f32[1,64,1,128]{3,1,2,0:T(8,128)S(1)} %get-tuple-element.14, f32[]{:T(128)} %multiply_reduce_fusion), kind=kLoop, calls=%fused_computation.8 | loop fusion | flops 73728 | bytes 196612 | tf_op jit(solution)/shard_map/div | solution.py:80
  (25 shorter events, 1.3 us)
Async XLA Ops:
  2.2 12.1 %copy-start.1 = (s32[2048]{0:T(1024)S(1)}, s32[2048]{0:T(1024)}, u32[]{:S(2)}) copy-start(s32[2048]{0:T(1024)} %param.5) | copy-start | bytes 24580
  2.2 25.5 %all-to-all-start = ((f32[32,24,128]{2,1,0:T(8,128)}), f32[32,24,128]{2,1,0:T(8,128)S(1)}, u32[]{:S(2)}, u32[]{:S(2)}) async-start(f32[32,24,128]{2,1,0:T(8,128)} %broadcast_in_dim.5), calls=%async_computation | async-start | bytes 786432 | tf_op jit(solution)/shard_map/all_to_all | solution.py:15
  14.4 0.7 copy-start.3
  15.0 0.7 copy-start.2
  75.3 0.7 copy-start
  76.0 14.6 %all-to-all-start.2 = ((f32[16,2,2,4,128]{4,0,2,1,3:T(8,128)}), f32[16,2,2,4,128]{4,0,2,1,3:T(8,128)S(1)}, u32[]{:S(2)}, u32[]{:S(2)}) async-start(f32[16,2,2,4,128]{4,0,2,1,3:T(8,128)} %copy.41), calls=%async_computation.2 | async-start | bytes 262144 | tf_op jit(solution)/shard_map/all_to_all | solution.py:202
